TPU v7x, 512 devices: a whole 4x4x16 slice. The times are simulated.
512 devices in a mesh: wide: 128 (over z, x, core), narrow: 4 (over y).
Axes of the slice: x: 4, y: 4, z: 16, core: 2. Of those that a mesh axis runs over, the one named last changes fastest.
Arguments:
- record: float32 [128, 128, 64, 128], P('wide', 'narrow'), may hold values from -6 to 6
Outputs:
- spectrum: float32 [2, 128, 4, 32, 64, 128], P(None, 'wide', 'narrow')
All inputs are finite; a program needn't handle non-finite values.
Results may differ from a plain program's by a relative error of at most 0.00007.
Values sent between devices are 32-bit elements; how exact they have to be, the bound alone decides.
No kernel may reach another device: no remote copies, remote signals or barrier semaphores. Data moves between devices by JAX's collectives and lax.ppermute only.
A program may use at most 64 MiB of HBM per device.

v0:
```python
import math

import jax
import jax.numpy as jnp
from jax import lax
from jax.sharding import PartitionSpec as P

PRECISE = lax.Precision.HIGHEST
TWO_PI = 2.0 * math.pi


def partner_2(block, axis, apart):
    count = lax.axis_size(axis)
    route = []
    for low in range(count):
        high = low | 1 << apart
        if high != low and high < count:
            route += [(low, high), (high, low)]
    return lax.ppermute(block, axis, route)


def block_table(inputs, outputs, length, factor):
    phases = inputs[:, None] * outputs[None, :] % length
    angles = phases.astype(jnp.float32) * (TWO_PI / length)
    cosine = jnp.cos(angles) * factor
    sines = jnp.sin(angles) * factor
    return jnp.stack([jnp.stack([cosine, sines]), jnp.stack([-sines, cosine])])


def rotate(values, angles):
    cosine = jnp.cos(angles)
    sines = jnp.sin(angles)
    return jnp.stack(
        [values[0] * cosine + values[1] * sines, values[1] * cosine - values[0] * sines]
    )


def reversed_digits(number, bit_count):
    result = 0 * number
    for position in range(bit_count):
        result = result + number // (1 << position) % 2 * (1 << bit_count - 1 - position)
    return result


def turn_mixed(values, frequency, cell_index, extent, length):
    offset = cell_index[:, None] * extent + jnp.arange(extent, dtype=jnp.int32)[None, :]
    phases = offset[None, :, :] * frequency[:, None, None] % length
    return rotate(values, phases.astype(jnp.float32) * (TWO_PI / length))


def first_factor(gathered, index_a, size_a, total_count):
    table_a = block_table(index_a, index_a, size_a, 1.0 / math.sqrt(total_count))[:, 0]
    return jnp.einsum("pak,arn->pkrn", table_a, gathered, precision=PRECISE)


def shards(record):
    local_a, local_b, size_c, size_d = record.shape
    wide_size = lax.axis_size("wide")
    narrow_size = lax.axis_size("narrow")
    levels = narrow_size.bit_length() - 1
    size_a = local_a * wide_size
    size_b = local_b * narrow_size
    total_count = size_a * size_b * size_c * size_d
    row_count = local_b * size_c
    row_share = row_count // wide_size
    wide_at = lax.axis_index("wide")
    narrow_at = lax.axis_index("narrow")
    index_a = jnp.arange(size_a, dtype=jnp.int32)
    third_index = jnp.arange(size_c, dtype=jnp.int32)
    inner_length = size_b * size_c * size_d
    row_index = narrow_at * row_count + wide_at * row_share + jnp.arange(row_share, dtype=jnp.int32)
    offset = row_index[:, None] * size_d + jnp.arange(size_d, dtype=jnp.int32)[None, :]
    phases = offset[None, :, :] * index_a[:, None, None] % total_count
    gathered = lax.all_to_all(
        record.reshape(local_a, row_count, size_d), "wide", split_axis=1, concat_axis=0, tiled=True
    )
    section_a = rotate(
        first_factor(gathered, index_a, size_a, total_count),
        phases.astype(jnp.float32) * (TWO_PI / total_count),
    )
    blocks = lax.all_to_all(section_a, "wide", split_axis=1, concat_axis=2, tiled=True).reshape(
        2, local_a, local_b, size_c, size_d
    )
    current = blocks
    for digit_place in reversed(range(levels)):
        partner = partner_2(current, "narrow", digit_place)
        upper_bit = narrow_at // (1 << digit_place) % 2
        current = partner + (1 - 2 * upper_bit).astype(jnp.float32) * current
        if digit_place > 0:
            lower_part = narrow_at % (1 << digit_place)
            current = rotate(
                current,
                (lower_part * upper_bit).astype(jnp.float32) * (TWO_PI / (2 << digit_place)),
            )
    residue = reversed_digits(narrow_at, levels)
    outputs_b = narrow_size * jnp.arange(local_b, dtype=jnp.int32) + residue
    table_b = block_table(jnp.arange(local_b, dtype=jnp.int32), outputs_b, size_b, 1.0)
    section_b = jnp.einsum("pqlm,qalcd->pamcd", table_b, current, precision=PRECISE)
    section_b = turn_mixed(section_b, outputs_b, third_index, size_d, inner_length)
    table_c = block_table(third_index, third_index, size_c, 1.0)
    section_c = jnp.einsum("pqck,qamcd->pamkd", table_c, section_b, precision=PRECISE)
    depth_index = jnp.arange(size_d, dtype=jnp.int32)
    phase_c = third_index[:, None] * depth_index[None, :] % (size_c * size_d)
    section_c = rotate(section_c, phase_c.astype(jnp.float32) * (TWO_PI / (size_c * size_d)))
    table_d = block_table(depth_index, depth_index, size_d, 1.0)
    section_d = jnp.einsum("pqdk,qamcd->pamck", table_d, section_c, precision=PRECISE)
    return section_d.reshape(2, local_a, 1, local_b, size_c, size_d)


def solution(mesh):
    return jax.shard_map(
        shards,
        mesh=mesh,
        in_specs=(P("wide", "narrow", None, None),),
        out_specs=P(None, "wide", "narrow", None, None, None),
        check_vma=False,
    )
```

profile of v0, /device:TPU:48, one launch (start us, length us, event | category | flops | bytes accessed | tf_op | source)
XLA Modules:
  0.0 309.7 jit_solution(11524176636607737341)
XLA Ops:
  0.0 19.0 %all-to-all-start = ((f32[1,2048,128]{2,0,1:T(1,128)}), f32[1,2048,128]{2,0,1:T(1,128)S(1)}, u32[]{:S(2)}, u32[]{:S(2)}) async-start(f32[1,2048,128]{2,0,1:T(1,128)} %bitcast.78), calls=%async_computation | async-start | bytes 2097152 | tf_op jit(solution)/shard_map/all_to_all | solution.py:74
  19.0 0.3 fusion.60
  19.3 0.3 broadcast_multiply_fusion
  19.6 0.1 iota_add_fusion.1
  19.7 54.8 %all-to-all-done = f32[1,2048,128]{2,0,1:T(1,128)S(1)} async-done(((f32[1,2048,128]{2,0,1:T(1,128)}), f32[1,2048,128]{2,0,1:T(1,128)S(1)}, u32[]{:S(2)}, u32[]{:S(2)}) %all-to-all-start) | async-done | bytes 1048608 | tf_op jit(solution)/shard_map/all_to_all | solution.py:74
  74.5 2.0 fusion.20
  76.5 4.4 %multiply_add_fusion.4 = (f32[1,128,16,128]{3,1,2,0:T(8,128)S(1)}, f32[1,128,16,128]{3,1,2,0:T(8,128)S(1)}) fusion(f32[2,128,16,128]{3,1,2,0:T(8,128)S(1)} %fusion.20, s32[16,128]{1,0:T(8,128)S(1)} %iota_add_fusion.1), kind=kLoop, calls=%fused_computation.40 | loop fusion | flops 5242880 | bytes 4202496 | tf_op jit(solution)/shard_map/add | solution.py:34
  80.9 0.2 pad_maximum_fusion
  81.1 1.2 copy.15
  82.3 104.6 %all_to_all.21 = f32[2,128,16,128]{3,2,0,1:T(8,128)S(1)} all-to-all(f32[2,128,16,128]{3,2,0,1:T(8,128)S(1)} %copy.15), channel_id=1, replica_groups=mesh['wide'=128,'narrow'=4] {'wide'}, dimensions={1} | all-to-all | bytes 4194304 | tf_op jit(solution)/shard_map/all_to_all | solution.py:81
  186.9 0.1 copy.16
  187.1 2.3 collective-permute-start
  189.5 49.4 %collective-permute-done = f32[2,1,32,64,128]{4,3,2,0,1:T(8,128)} collective-permute-done((f32[2,1,32,64,128]{4,3,2,0,1:T(8,128)S(1)}, f32[2,1,32,64,128]{4,3,2,0,1:T(8,128)}, u32[]{:S(2)}, u32[]{:S(2)}) %collective-permute-start) | collective-permute-done | bytes 2097184 | tf_op jit(solution)/shard_map/ppermute | solution.py:19
  239.0 2.0 multiply_add_fusion
  241.0 0.3 multiply_add_fusion.3
  241.3 1.5 pad_maximum_fusion.1
  242.7 3.4 %collective-permute-start.1 = (f32[2,1,32,64,128]{4,3,2,0,1:T(8,128)}, f32[2,1,32,64,128]{4,3,2,0,1:T(8,128)}, u32[]{:S(2)}, u32[]{:S(2)}) collective-permute-start(f32[2,1,32,64,128]{4,3,2,0,1:T(8,128)} %pad_maximum_fusion.1), channel_id=1, source_target_pairs={{0,1},{1,0},{2,3},{3,2},{4,5},{5,4},{6,7},{7,6},{8,9},{9,8},{10,11... | collective-permute-start | bytes 6291464 | tf_op jit(solution)/shard_map/ppermute | solution.py:19
  246.1 0.1 fusion.71
  246.3 0.1 fusion.66
  246.4 0.1 fusion.64
  246.6 0.3 fusion.57
  246.8 0.2 fusion.72
  247.0 0.3 fusion.55
  247.3 0.1 iota_add_fusion
  247.4 45.2 %collective-permute-done.1 = f32[2,1,32,64,128]{4,3,2,0,1:T(8,128)} collective-permute-done((f32[2,1,32,64,128]{4,3,2,0,1:T(8,128)}, f32[2,1,32,64,128]{4,3,2,0,1:T(8,128)}, u32[]{:S(2)}, u32[]{:S(2)}) %collective-permute-start.1) | collective-permute-done | bytes 2097184 | tf_op jit(solution)/shard_map/ppermute | solution.py:19
  292.6 2.0 add_bitcast_fusion
  294.6 3.3 %fusion.7 = f32[2,1,32,64,128]{4,2,0,3,1:T(8,128)S(1)} fusion(f32[2,32,64,128,1]{3,2,1,0,4:T(8,128)S(1)} %add_bitcast_fusion, f32[1,2,32,32]{2,3,1,0:T(8,128)S(1)} %get-tuple-element.20, f32[1,2,32,32]{2,3,1,0:T(8,128)S(1)} %get-tuple-element.19), kind=kOutput, calls=%fused_computation.16 | convolution fusion | flops 402657280 | bytes 4210688 | tf_op jit(solution)/shard_map/pqlm,qalcd->pamcd/dot_general | solution.py:98
  297.9 4.4 %multiply_add_fusion.2 = (f32[1,1,32,64,128]{4,2,0,3,1:T(8,128)S(1)}, f32[1,1,32,64,128]{4,2,0,3,1:T(8,128)S(1)}) fusion(f32[2,1,32,64,128]{4,2,0,3,1:T(8,128)S(1)} %fusion.7, s32[32]{0:T(128)S(1)} %multiply_add_fusion.5, s32[64,128]{1,0:T(8,128)S(1)} %iota_add_fusion), kind=kLoop, calls=%fused_computation.36 | loop fusion | flops 5242880 | bytes 4227200 | tf_op jit(solution)/shard_map/add | solution.py:34
  302.4 0.2 maximum_bitcast_fusion
  302.6 3.2 %fusion.10 = f32[2,1,32,64,128]{4,3,0,2,1:T(8,128)S(1)} fusion(f32[2,32,64,128,1]{3,1,0,2,4:T(8,128)S(1)} %maximum_bitcast_fusion, f32[1,2,64,64]{2,3,1,0:T(8,128)S(1)} %get-tuple-element.18, f32[1,2,64,64]{2,3,1,0:T(8,128)S(1)} %get-tuple-element.17), kind=kOutput, calls=%fused_computation.17 | convolution fusion | flops 805322752 | bytes 4259840 | tf_op jit(solution)/shard_map/pqck,qamcd->pamkd/dot_general | solution.py:101
  305.9 0.4 multiply_add_fusion.1
  306.3 1.9 fusion.13
  308.2 1.5 copy.20
  (7 shorter events, 0.1 us)
Async XLA Ops:
  0.0 74.5 %all-to-all-start = ((f32[1,2048,128]{2,0,1:T(1,128)}), f32[1,2048,128]{2,0,1:T(1,128)S(1)}, u32[]{:S(2)}, u32[]{:S(2)}) async-start(f32[1,2048,128]{2,0,1:T(1,128)} %bitcast.78), calls=%async_computation | async-start | bytes 2097152 | tf_op jit(solution)/shard_map/all_to_all | solution.py:74
  187.1 51.9 %collective-permute-start = (f32[2,1,32,64,128]{4,3,2,0,1:T(8,128)S(1)}, f32[2,1,32,64,128]{4,3,2,0,1:T(8,128)}, u32[]{:S(2)}, u32[]{:S(2)}) collective-permute-start(f32[2,1,32,64,128]{4,3,2,0,1:T(8,128)S(1)} %bitcast.75), channel_id=1, source_target_pairs={{0,2},{2,0},{1,3},{3,1},{4,6},{6,4},{5,7},{7,5},{8,10},{10,8},{9,1... | collective-permute-start | bytes 6291464 | tf_op jit(solution)/shard_map/ppermute | solution.py:19
  242.7 49.8 %collective-permute-start.1 = (f32[2,1,32,64,128]{4,3,2,0,1:T(8,128)}, f32[2,1,32,64,128]{4,3,2,0,1:T(8,128)}, u32[]{:S(2)}, u32[]{:S(2)}) collective-permute-start(f32[2,1,32,64,128]{4,3,2,0,1:T(8,128)} %pad_maximum_fusion.1), channel_id=1, source_target_pairs={{0,1},{1,0},{2,3},{3,2},{4,5},{5,4},{6,7},{7,6},{8,9},{9,8},{10,11... | collective-permute-start | bytes 6291464 | tf_op jit(solution)/shard_map/ppermute | solution.py:19
where the time goes:
time: 310 us
  waiting for transfers between devices  149 us (48%)
  blocking collectives  105 us (34%)
  starting transfers between devices  24.6 us (8%)
  other arithmetic  17.4 us (6%)
  matrix products  10.5 us (3%)
    all_to_all x1, blocking collectives, shards(): lax.all_to_all(section_a, 'wide', split_axis=1, concat_axis=2, tiled=True)  105 us
    ppermute x2, waiting for transfers between devices, partner_2(): return lax.ppermute(block, axis, route)  94.6 us
    all_to_all x1, waiting for transfers between devices, shards(): lax.all_to_all(record.reshape(local_a, row_count, size_d), 'wide', split_...  54.8 us
    all_to_all x1, starting transfers between devices, shards(): lax.all_to_all(record.reshape(local_a, row_count, size_d), 'wide', split_...  19 us
    add x4, other arithmetic, rotate(): values[0] * cosine + values[1] * sines  9.56 us
  transfers between devices with their start and end apart: 3, of which 3 were waited for; matrix products, arithmetic and copies ran while one was open for 1% of the time, Pallas kernels for 0%

commit v1 on v0

v1 whole, which is shorter than its diff:
```python
import math

import jax
import jax.numpy as jnp
from jax import lax
from jax.sharding import PartitionSpec as P

PRECISE = lax.Precision.HIGHEST
TWO_PI = 2.0 * math.pi
DEVICES = ("wide", "narrow")


def reversed_digits(number, bit_count):
    result = 0 * number
    for position in range(bit_count):
        result = result + number // (1 << position) % 2 * (1 << bit_count - 1 - position)
    return result


def unit_turn(phases, length):
    angles = phases.astype(jnp.float32) * (TWO_PI / length)
    return jnp.cos(angles), jnp.sin(angles)


def rotate(values, phases, length):
    cosine, sines = unit_turn(phases, length)
    return jnp.stack(
        [values[0] * cosine + values[1] * sines, values[1] * cosine - values[0] * sines]
    )


def block_table(inputs, outputs, length, factor):
    cosine, sines = unit_turn(inputs[:, None] * outputs[None, :] % length, length)
    cosine = cosine * factor
    sines = sines * factor
    return jnp.stack([jnp.stack([cosine, sines]), jnp.stack([-sines, cosine])])


def shards(record):
    local_a, local_b, size_c, size_d = record.shape
    wide_size = lax.axis_size("wide")
    narrow_size = lax.axis_size("narrow")
    levels = narrow_size.bit_length() - 1
    size_a = local_a * wide_size
    size_b = local_b * narrow_size
    total_count = size_a * size_b * size_c * size_d
    groups = wide_size * narrow_size
    column_count = local_b * size_c * size_d
    columns = column_count // groups
    here = lax.axis_index(DEVICES)

    gathered = lax.all_to_all(
        record.reshape(groups, columns), DEVICES, split_axis=0, concat_axis=0, tiled=True
    )
    slots = jnp.arange(groups, dtype=jnp.int32)
    frequency = slots // narrow_size + size_a * reversed_digits(slots % narrow_size, levels)
    sources = jnp.arange(groups, dtype=jnp.int32)
    table = block_table(sources, frequency, groups, 1.0 / math.sqrt(total_count))[:, 0]
    section = jnp.einsum("pak,an->pkn", table, gathered, precision=PRECISE)
    column_index = here * columns + jnp.arange(columns, dtype=jnp.int32)
    section = rotate(section, frequency[:, None] * column_index[None, :] % total_count, total_count)
    owned = lax.all_to_all(section, DEVICES, split_axis=1, concat_axis=1, tiled=True)
    values = owned.reshape(2, local_b, size_c * size_d)

    index_b = jnp.arange(local_b, dtype=jnp.int32)
    table_b = block_table(index_b, index_b, local_b, 1.0)
    values = jnp.einsum("pqlm,qle->pme", table_b, values, precision=PRECISE)
    inner = jnp.arange(size_c * size_d, dtype=jnp.int32)
    values = rotate(values, index_b[:, None] * inner[None, :] % column_count, column_count)
    values = values.reshape(2, local_b, size_c, size_d)
    index_c = jnp.arange(size_c, dtype=jnp.int32)
    table_c = block_table(index_c, index_c, size_c, 1.0)
    values = jnp.einsum("pqck,qmcd->pmkd", table_c, values, precision=PRECISE)
    index_d = jnp.arange(size_d, dtype=jnp.int32)
    values = rotate(
        values, (index_c[:, None] * index_d[None, :] % (size_c * size_d))[None], size_c * size_d
    )
    table_d = block_table(index_d, index_d, size_d, 1.0)
    values = jnp.einsum("pqdk,qmcd->pmck", table_d, values, precision=PRECISE)
    return values.reshape(2, 1, 1, local_b, size_c, size_d)


def solution(mesh):
    return jax.shard_map(
        shards,
        mesh=mesh,
        in_specs=(P("wide", "narrow", None, None),),
        out_specs=P(None, "wide", "narrow", None, None, None),
        check_vma=False,
    )
```

time: 310 us -> 221 us (0.71)
  the two profiles are of different devices: /device:TPU:48 before, /device:TPU:1 now
where the time goes in v1:
time: 221 us
  waiting for transfers between devices  152 us (69%)
  starting transfers between devices  32.9 us (15%)
  other arithmetic  17.1 us (8%)
  matrix products  10.6 us (5%)
  local copies, waits for them, and re-layouts  7.9 us (4%)
    all_to_all x1, waiting for transfers between devices, shards(): lax.all_to_all(section, DEVICES, split_axis=1, concat_axis=1, tiled=True)  100 us
    all_to_all x1, waiting for transfers between devices, shards(): lax.all_to_all(record.reshape(groups, columns), DEVICES, split_axis=0, co...  52.4 us
    all_to_all x1, starting transfers between devices, shards(): lax.all_to_all(record.reshape(groups, columns), DEVICES, split_axis=0, co...  24.3 us
    all_to_all x1, starting transfers between devices, shards(): lax.all_to_all(section, DEVICES, split_axis=1, concat_axis=1, tiled=True)  8.6 us
    add x2, other arithmetic, rotate(): values[0] * cosine + values[1] * sines  5.08 us
    dot_general x1, matrix products, shards(): section = jnp.einsum('pak,an->pkn', table, gathered, precision=PRECISE)  4.77 us
  transfers between devices with their start and end apart: 2, of which 2 were waited for; matrix products, arithmetic and copies ran while one was open for 3% of the time, Pallas kernels for 0%

profile of v1, /device:TPU:1, one launch (start us, length us, event | category | flops | bytes accessed | tf_op | source)
XLA Modules:
  0.0 221.1 jit_solution(13749317693440980046)
XLA Ops:
  0.0 24.3 %all-to-all-start = ((f32[512,1,512]{2,1,0:T(1,128)}), f32[512,1,512]{2,1,0:T(1,128)S(1)}, u32[]{:S(2)}, u32[]{:S(2)}) async-start(f32[512,1,512]{2,1,0:T(1,128)} %bitcast.81), calls=%async_computation | async-start | bytes 2097152 | tf_op jit(solution)/shard_map/all_to_all | solution.py:52
  24.3 4.3 %sine_multiply_fusion = (f32[1,512,512]{1,2,0:T(8,128)S(1)}, f32[1,512,512]{1,2,0:T(8,128)S(1)}, f32[1,512,512]{1,2,0:T(8,128)S(1)}) fusion(s32[512]{0:T(512)S(1)} %get-tuple-element.22), kind=kLoop, calls=%fused_computation.50 | loop fusion | flops 4456448 | bytes 3147776 | tf_op jit(solution)/shard_map/mul | solution.py:35
  28.6 1.9 maximum_bitcast_fusion
  30.5 52.4 %all-to-all-done = f32[512,1,512]{2,1,0:T(1,128)S(1)} async-done(((f32[512,1,512]{2,1,0:T(1,128)}), f32[512,1,512]{2,1,0:T(1,128)S(1)}, u32[]{:S(2)}, u32[]{:S(2)}) %all-to-all-start) | async-done | bytes 1048608 | tf_op jit(solution)/shard_map/all_to_all | solution.py:52
  82.9 4.8 %fusion.1 = f32[2,512,512]{1,2,0:T(8,128)S(1)} fusion(f32[1,2,512,512]{2,3,0,1:T(8,128)} %get-tuple-element.12, f32[1,2,512,512]{2,3,0,1:T(8,128)S(1)} %get-tuple-element.11, f32[512,1,512]{2,1,0:T(1,128)S(1)} %all-to-all-done), kind=kOutput, calls=%fused_computation.3 | convolution fusion | flops 3221749760 | bytes 7340032 | tf_op jit(solution)/shard_map/pak,an->pkn/dot_general | solution.py:59
  87.7 4.7 %multiply_add_fusion.1 = (f32[1,512,512]{1,2,0:T(8,128)S(1)}, f32[1,512,512]{1,2,0:T(8,128)S(1)}) fusion(f32[2,512,512]{1,2,0:T(8,128)S(1)} %fusion.1, s32[512]{0:T(512)S(1)} %get-tuple-element.23, s32[512]{0:T(512)S(1)} %get-tuple-element.22), kind=kLoop, calls=%fused_computation.49 | loop fusion | flops 5242880 | bytes 4198400 | tf_op jit(solution)/shard_map/add | solution.py:28
  92.4 0.2 pad_maximum_fusion.1
  92.6 2.4 %copy.18 = f32[2,512,512]{2,0,1:T(2,128)} copy(f32[2,512,512]{1,2,0:T(8,128)S(1)} %pad_maximum_fusion.1) | data formatting | bytes 4194304 | tf_op jit(solution)/shard_map/stack | solution.py:27
  95.0 8.6 %all-to-all-start.1 = ((f32[2,512,512]{2,0,1:T(2,128)}), f32[2,512,512]{2,0,1:T(2,128)S(1)}, u32[]{:S(2)}, u32[]{:S(2)}) async-start(f32[2,512,512]{2,0,1:T(2,128)} %copy.18), calls=%async_computation.1 | async-start | bytes 4194304 | tf_op jit(solution)/shard_map/all_to_all | solution.py:62
  103.6 0.1 fusion.75
  103.7 0.1 fusion.73
  103.8 0.1 fusion.72
  103.9 0.1 fusion.67
  104.1 0.1 fusion.65
  104.2 0.3 fusion.61
  104.5 0.3 fusion.53
  104.8 100.1 %all-to-all-done.1 = f32[2,512,512]{2,0,1:T(2,128)S(1)} async-done(((f32[2,512,512]{2,0,1:T(2,128)}), f32[2,512,512]{2,0,1:T(2,128)S(1)}, u32[]{:S(2)}, u32[]{:S(2)}) %all-to-all-start.1) | async-done | bytes 2097184 | tf_op jit(solution)/shard_map/all_to_all | solution.py:62
  204.9 1.7 copy.19
  206.6 1.7 reshape.744
  208.3 1.9 convolution_bitcast_fusion
  210.3 4.4 %add_bitcast_fusion = (f32[4,8,64,128]{3,1,2,0:T(8,128)S(1)}, f32[4,8,64,128]{3,1,2,0:T(8,128)S(1)}) fusion(f32[2,32,8192]{2,1,0:T(8,128)S(1)} %convolution_bitcast_fusion), kind=kLoop, calls=%fused_computation.45 | loop fusion | flops 5242880 | bytes 4194304
  214.7 0.2 copy.31
  214.9 0.1 bitcast_bitcast_fusion
  215.0 0.2 copy.30
  215.2 0.1 bitcast_bitcast_fusion.1
  215.3 2.0 fusion.11
  217.3 0.4 multiply_add_fusion
  217.8 1.9 fusion.10
  219.7 1.5 copy.22
  (4 shorter events, 0.1 us)
Async XLA Ops:
  0.0 82.9 %all-to-all-start = ((f32[512,1,512]{2,1,0:T(1,128)}), f32[512,1,512]{2,1,0:T(1,128)S(1)}, u32[]{:S(2)}, u32[]{:S(2)}) async-start(f32[512,1,512]{2,1,0:T(1,128)} %bitcast.81), calls=%async_computation | async-start | bytes 2097152 | tf_op jit(solution)/shard_map/all_to_all | solution.py:52
  95.0 109.9 %all-to-all-start.1 = ((f32[2,512,512]{2,0,1:T(2,128)}), f32[2,512,512]{2,0,1:T(2,128)S(1)}, u32[]{:S(2)}, u32[]{:S(2)}) async-start(f32[2,512,512]{2,0,1:T(2,128)} %copy.18), calls=%async_computation.1 | async-start | bytes 4194304 | tf_op jit(solution)/shard_map/all_to_all | solution.py:62

commit v2 on v1

--- a/solution.py
+++ b/solution.py
@@ -59,12 +59,14 @@
     section = jnp.einsum("pak,an->pkn", table, gathered, precision=PRECISE)
     column_index = here * columns + jnp.arange(columns, dtype=jnp.int32)
     section = rotate(section, frequency[:, None] * column_index[None, :] % total_count, total_count)
-    owned = lax.all_to_all(section, DEVICES, split_axis=1, concat_axis=1, tiled=True)
-    values = owned.reshape(2, local_b, size_c * size_d)
+    section = jnp.transpose(section, (1, 0, 2))
+    owned = lax.all_to_all(section, DEVICES, split_axis=0, concat_axis=0, tiled=True)
+    values = owned.reshape(local_b, groups // local_b, 2, columns)
 
     index_b = jnp.arange(local_b, dtype=jnp.int32)
     table_b = block_table(index_b, index_b, local_b, 1.0)
-    values = jnp.einsum("pqlm,qle->pme", table_b, values, precision=PRECISE)
+    values = jnp.einsum("pqlm,lhqt->pmht", table_b, values, precision=PRECISE)
+    values = values.reshape(2, local_b, size_c * size_d)
     inner = jnp.arange(size_c * size_d, dtype=jnp.int32)
     values = rotate(values, index_b[:, None] * inner[None, :] % column_count, column_count)
     values = values.reshape(2, local_b, size_c, size_d)

time: 221 us -> 221 us (level)
  local copies, waits for them, and re-layouts: 7.9 us -> 5.51 us
    add x2 -> x3, other arithmetic: 5.08 us -> 10 us  [rotate(): values[0] * cosine + values[1] * sines]
    unnamed x1 -> x0, other arithmetic: 4.41 us -> none
    another operation x3 -> x0, local copies, waits for them, and re-layouts: 2.62 us -> none  [rotate(): jnp.stack([values[0] * cosine + values[1] * sines, values[1] * cosine - v...]
    transpose x0 -> x1, local copies, waits for them, and re-layouts: none -> 2.43 us  [shards(): section = jnp.transpose(section, (1, 0, 2))]
  transfers between devices with their start and end apart: 2 -> 2, of which waited for: 2 -> 2; matrix products, arithmetic and copies ran while one was open for 3% -> 4% of each run, Pallas kernels for 0% -> 0%
where the time goes in v2:
time: 221 us; the launch traced here: 220 us
  waiting for transfers between devices  151 us (68%)
  starting transfers between devices  32.9 us (15%)
  other arithmetic  18.8 us (9%)
  matrix products  11.7 us (5%)
  local copies, waits for them, and re-layouts  5.51 us (2%)
    all_to_all x1, waiting for transfers between devices, shards(): lax.all_to_all(section, DEVICES, split_axis=0, concat_axis=0, tiled=True)  98.8 us
    all_to_all x1, waiting for transfers between devices, shards(): lax.all_to_all(record.reshape(groups, columns), DEVICES, split_axis=0, co...  52.4 us
    all_to_all x1, starting transfers between devices, shards(): lax.all_to_all(record.reshape(groups, columns), DEVICES, split_axis=0, co...  24.3 us
    add x3, other arithmetic, rotate(): values[0] * cosine + values[1] * sines  10 us
    all_to_all x1, starting transfers between devices, shards(): lax.all_to_all(section, DEVICES, split_axis=0, concat_axis=0, tiled=True)  8.6 us
    dot_general x1, matrix products, shards(): section = jnp.einsum('pak,an->pkn', table, gathered, precision=PRECISE)  4.77 us
  transfers between devices with their start and end apart: 2, of which 2 were waited for; matrix products, arithmetic and copies ran while one was open for 4% of the time, Pallas kernels for 0%

profile of v2, /device:TPU:1, one launch (start us, length us, event | category | flops | bytes accessed | tf_op | source)
XLA Modules:
  0.0 220.4 jit_solution(1034358435221196390)
XLA Ops:
  0.0 24.3 %all-to-all-start = ((f32[512,1,512]{2,1,0:T(1,128)}), f32[512,1,512]{2,1,0:T(1,128)S(1)}, u32[]{:S(2)}, u32[]{:S(2)}) async-start(f32[512,1,512]{2,1,0:T(1,128)} %bitcast.94), calls=%async_computation | async-start | bytes 2097152 | tf_op jit(solution)/shard_map/all_to_all | solution.py:52
  24.3 4.3 %sine_multiply_fusion = (f32[1,512,512]{1,2,0:T(8,128)S(1)}, f32[1,512,512]{1,2,0:T(8,128)S(1)}, f32[1,512,512]{1,2,0:T(8,128)S(1)}) fusion(s32[512]{0:T(512)S(1)} %get-tuple-element.24), kind=kLoop, calls=%fused_computation.55 | loop fusion | flops 4456448 | bytes 3147776 | tf_op jit(solution)/shard_map/mul | solution.py:35
  28.6 1.9 maximum_bitcast_fusion
  30.5 52.4 %all-to-all-done = f32[512,1,512]{2,1,0:T(1,128)S(1)} async-done(((f32[512,1,512]{2,1,0:T(1,128)}), f32[512,1,512]{2,1,0:T(1,128)S(1)}, u32[]{:S(2)}, u32[]{:S(2)}) %all-to-all-start) | async-done | bytes 1048608 | tf_op jit(solution)/shard_map/all_to_all | solution.py:52
  82.9 4.8 %fusion.1 = f32[2,512,512]{1,2,0:T(8,128)S(1)} fusion(f32[1,2,512,512]{2,3,0,1:T(8,128)} %get-tuple-element.14, f32[1,2,512,512]{2,3,0,1:T(8,128)S(1)} %get-tuple-element.13, f32[512,1,512]{2,1,0:T(1,128)S(1)} %all-to-all-done), kind=kOutput, calls=%fused_computation.2 | convolution fusion | flops 3221749760 | bytes 7340032 | tf_op jit(solution)/shard_map/pak,an->pkn/dot_general | solution.py:59
  87.7 4.7 %multiply_add_fusion.1 = (f32[1,512,512]{1,2,0:T(8,128)S(1)}, f32[1,512,512]{1,2,0:T(8,128)S(1)}) fusion(f32[2,512,512]{1,2,0:T(8,128)S(1)} %fusion.1, s32[512]{0:T(512)S(1)} %get-tuple-element.25, s32[512]{0:T(512)S(1)} %get-tuple-element.24), kind=kLoop, calls=%fused_computation.54 | loop fusion | flops 5242880 | bytes 4198400 | tf_op jit(solution)/shard_map/add | solution.py:28
  92.4 0.2 maximum_bitcast_fusion.2
  92.6 2.4 %copy.22 = f32[512,2,512]{2,1,0:T(2,128)} copy(f32[512,2,512]{0,2,1:T(8,128)S(1)} %maximum_bitcast_fusion.2) | data formatting | bytes 4194304 | tf_op jit(solution)/shard_map/transpose | solution.py:62
  95.0 8.6 %all-to-all-start.1 = ((f32[512,2,512]{2,1,0:T(2,128)}), f32[512,2,512]{2,1,0:T(2,128)S(1)}, u32[]{:S(2)}, u32[]{:S(2)}) async-start(f32[512,2,512]{2,1,0:T(2,128)} %copy.22), calls=%async_computation.1 | async-start | bytes 4194304 | tf_op jit(solution)/shard_map/all_to_all | solution.py:63
  103.6 0.1 fusion.82
  103.7 0.1 fusion.80
  103.8 0.6 multiply_add_fusion.2
  104.4 0.1 fusion.79
  104.5 0.1 fusion.74
  104.7 0.8 fusion.72
  105.5 0.3 fusion.68
  105.7 0.3 fusion.60
  106.1 98.8 %all-to-all-done.1 = f32[512,2,512]{2,1,0:T(2,128)S(1)} async-done(((f32[512,2,512]{2,1,0:T(2,128)}), f32[512,2,512]{2,1,0:T(2,128)S(1)}, u32[]{:S(2)}, u32[]{:S(2)}) %all-to-all-start.1) | async-done | bytes 2097184 | tf_op jit(solution)/shard_map/all_to_all | solution.py:63
  204.9 3.1 %fusion.13 = f32[2,32,16,512]{3,1,2,0:T(8,128)S(1)} fusion(f32[32,16,2,512]{3,2,1,0:T(2,128)S(1)} %bitcast.93, f32[1,2,32,32]{2,3,1,0:T(8,128)S(1)} %get-tuple-element.20, f32[1,2,32,32]{2,3,1,0:T(8,128)S(1)} %get-tuple-element.19), kind=kOutput, calls=%fused_computation.21 | convolution fusion | flops 402657280 | bytes 4210688 | tf_op jit(solution)/shard_map/pqlm,lhqt->pmht/dot_general | solution.py:68
  208.0 0.3 fusion.101
  208.2 0.6 copy.25
  208.8 0.1 squeeze.7
  208.9 0.6 copy.27
  209.5 0.1 squeeze.8
  209.6 5.0 %fusion.29 = (f32[1,32,64,128]{3,2,0,1:T(8,128)S(1)}, f32[1,32,64,128]{3,2,0,1:T(8,128)S(1)}) fusion(f32[1,32,64,128]{3,2,1,0:T(8,128)S(1)} %squeeze.8, f32[1,32,64,128]{3,2,1,0:T(8,128)S(1)} %squeeze.7, s32[64,128]{1,0:T(8,128)} %multiply_add_fusion.2), kind=kLoop, calls=%fused_computation.45 | loop fusion | flops 5242880 | bytes 4227072 | tf_op jit(solution)/shard_map/add | solution.py:28
  214.6 0.0 copy-start
  214.6 0.0 copy-start.1
  214.6 2.0 fusion.17
  216.6 0.0 copy-done
  216.6 0.0 copy-done.1
  216.6 0.4 multiply_add_fusion
  217.1 1.9 fusion.16
  219.0 1.5 copy.31
  (4 shorter events, 0.1 us)
Async XLA Ops:
  0.0 82.9 %all-to-all-start = ((f32[512,1,512]{2,1,0:T(1,128)}), f32[512,1,512]{2,1,0:T(1,128)S(1)}, u32[]{:S(2)}, u32[]{:S(2)}) async-start(f32[512,1,512]{2,1,0:T(1,128)} %bitcast.94), calls=%async_computation | async-start | bytes 2097152 | tf_op jit(solution)/shard_map/all_to_all | solution.py:52
  95.0 109.9 %all-to-all-start.1 = ((f32[512,2,512]{2,1,0:T(2,128)}), f32[512,2,512]{2,1,0:T(2,128)S(1)}, u32[]{:S(2)}, u32[]{:S(2)}) async-start(f32[512,2,512]{2,1,0:T(2,128)} %copy.22), calls=%async_computation.1 | async-start | bytes 4194304 | tf_op jit(solution)/shard_map/all_to_all | solution.py:63
  214.6 2.0 copy-start
  214.6 2.0 copy-start.1

commit v3 on v1

--- a/solution.py
+++ b/solution.py
@@ -22,18 +22,15 @@
     return jnp.cos(angles), jnp.sin(angles)
 
 
-def rotate(values, phases, length):
-    cosine, sines = unit_turn(phases, length)
-    return jnp.stack(
-        [values[0] * cosine + values[1] * sines, values[1] * cosine - values[0] * sines]
-    )
-
-
 def block_table(inputs, outputs, length, factor):
     cosine, sines = unit_turn(inputs[:, None] * outputs[None, :] % length, length)
     cosine = cosine * factor
     sines = sines * factor
     return jnp.stack([jnp.stack([cosine, sines]), jnp.stack([-sines, cosine])])
+
+
+def turn(values, cosine, sines):
+    return values[0] * cosine + values[1] * sines, values[1] * cosine - values[0] * sines
 
 
 def shards(record):
@@ -54,28 +51,34 @@
     )
     slots = jnp.arange(groups, dtype=jnp.int32)
     frequency = slots // narrow_size + size_a * reversed_digits(slots % narrow_size, levels)
-    sources = jnp.arange(groups, dtype=jnp.int32)
-    table = block_table(sources, frequency, groups, 1.0 / math.sqrt(total_count))[:, 0]
-    section = jnp.einsum("pak,an->pkn", table, gathered, precision=PRECISE)
+    cosine, sines = unit_turn(frequency[:, None] * slots[None, :] % groups, groups)
+    scale = 1.0 / math.sqrt(total_count)
+    table = jnp.stack([cosine * scale, -sines * scale], axis=1).reshape(2 * groups, groups)
     column_index = here * columns + jnp.arange(columns, dtype=jnp.int32)
-    section = rotate(section, frequency[:, None] * column_index[None, :] % total_count, total_count)
-    owned = lax.all_to_all(section, DEVICES, split_axis=1, concat_axis=1, tiled=True)
-    values = owned.reshape(2, local_b, size_c * size_d)
+    twiddle = unit_turn(frequency[:, None] * column_index[None, :] % total_count, total_count)
+    gathered, table, twiddle = lax.optimization_barrier((gathered, table, twiddle))
+    section = jnp.dot(table, gathered, precision=PRECISE).reshape(groups, 2, columns)
+    section = jnp.stack(turn((section[:, 0], section[:, 1]), *twiddle), axis=1)
+    owned = lax.all_to_all(section, DEVICES, split_axis=0, concat_axis=0, tiled=True)
 
     index_b = jnp.arange(local_b, dtype=jnp.int32)
     table_b = block_table(index_b, index_b, local_b, 1.0)
-    values = jnp.einsum("pqlm,qle->pme", table_b, values, precision=PRECISE)
     inner = jnp.arange(size_c * size_d, dtype=jnp.int32)
-    values = rotate(values, index_b[:, None] * inner[None, :] % column_count, column_count)
-    values = values.reshape(2, local_b, size_c, size_d)
+    twiddle_b = unit_turn(index_b[:, None] * inner[None, :] % column_count, column_count)
     index_c = jnp.arange(size_c, dtype=jnp.int32)
     table_c = block_table(index_c, index_c, size_c, 1.0)
+    index_d = jnp.arange(size_d, dtype=jnp.int32)
+    twiddle_c = unit_turn(index_c[:, None] * index_d[None, :] % (size_c * size_d), size_c * size_d)
+    table_d = block_table(index_d, index_d, size_d, 1.0)
+    owned, table_b, twiddle_b, table_c, twiddle_c, table_d = lax.optimization_barrier(
+        (owned, table_b, twiddle_b, table_c, twiddle_c, table_d)
+    )
+    values = owned.reshape(local_b, groups // local_b, 2, columns)
+    values = jnp.einsum("pqlm,lhqt->pmht", table_b, values, precision=PRECISE)
+    values = values.reshape(2, local_b, size_c * size_d)
+    values = jnp.stack(turn(values, *twiddle_b)).reshape(2, local_b, size_c, size_d)
     values = jnp.einsum("pqck,qmcd->pmkd", table_c, values, precision=PRECISE)
-    index_d = jnp.arange(size_d, dtype=jnp.int32)
-    values = rotate(
-        values, (index_c[:, None] * index_d[None, :] % (size_c * size_d))[None], size_c * size_d
-    )
-    table_d = block_table(index_d, index_d, size_d, 1.0)
+    values = jnp.stack(turn(values, twiddle_c[0][None], twiddle_c[1][None]))
     values = jnp.einsum("pqdk,qmcd->pmck", table_d, values, precision=PRECISE)
     return values.reshape(2, 1, 1, local_b, size_c, size_d)
 

time: 221 us -> 220 us (level)
  waiting for transfers between devices: 152 us -> 136 us
  local copies, waits for them, and re-layouts: 7.9 us -> 15.1 us
  other arithmetic: 17.1 us -> 22.6 us
    sin x4 -> x6, other arithmetic: 0.65 us -> 12.5 us  [unit_turn(): return (jnp.cos(angles), jnp.sin(angles))]
    all_to_all x1, waiting for transfers between devices: 52.4 us -> 42.6 us  [shards(): lax.all_to_all(record.reshape(groups, columns), DEVICES, split_axis=0, co...]
    all_to_all x1, waiting for transfers between devices: 100 us -> 93.2 us  [shards(): lax.all_to_all(section, DEVICES, split_axis=0, concat_axis=0, tiled=True)]
    add x2 -> x1, other arithmetic: 5.08 us -> 0.42 us  [turn(): values[0] * cosine + values[1] * sines]
    unnamed x1, other arithmetic: 4.41 us -> 0.25 us
    another operation x1 -> x3, other arithmetic: 0.17 us -> 3.96 us  [the longest x2 3.79 us: shards(): section = jnp.stack(turn((section[:, 0], section[:, 1]), *twiddle), axis=1)]
    reshape x1 -> x2, local copies, waits for them, and re-layouts: 1.75 us -> 5.4 us  [the longest x1 2.71 us: shards(): jnp.dot(table, gathered, precision=PRECISE).reshape(groups, 2, columns)]
  transfers between devices with their start and end apart: 2 -> 2, of which waited for: 2 -> 2; matrix products, arithmetic and copies ran while one was open for 3% -> 11% of each run, Pallas kernels for 0% -> 0%
where the time goes in v3:
time: 220 us; the launch traced here: 219 us
  waiting for transfers between devices  136 us (62%)
  starting transfers between devices  33 us (15%)
  other arithmetic  22.6 us (10%)
  local copies, waits for them, and re-layouts  15.1 us (7%)
  matrix products  12.6 us (6%)
    all_to_all x1, waiting for transfers between devices, shards(): lax.all_to_all(section, DEVICES, split_axis=0, concat_axis=0, tiled=True)  93.2 us
    all_to_all x1, waiting for transfers between devices, shards(): lax.all_to_all(record.reshape(groups, columns), DEVICES, split_axis=0, co...  42.6 us
    all_to_all x1, starting transfers between devices, shards(): lax.all_to_all(record.reshape(groups, columns), DEVICES, split_axis=0, co...  24.3 us
    sin x6, other arithmetic, unit_turn(): return (jnp.cos(angles), jnp.sin(angles))  12.5 us
    all_to_all x1, starting transfers between devices, shards(): lax.all_to_all(section, DEVICES, split_axis=0, concat_axis=0, tiled=True)  8.64 us
    dot_general x1, matrix products, shards(): jnp.dot(table, gathered, precision=PRECISE).reshape(groups, 2, columns)  4.76 us
  transfers between devices with their start and end apart: 2, of which 2 were waited for; matrix products, arithmetic and copies ran while one was open for 11% of the time, Pallas kernels for 0%

profile of v3, /device:TPU:1, one launch (start us, length us, event | category | flops | bytes accessed | tf_op | source)
XLA Modules:
  0.0 219.4 jit_solution(2075032067774349509)
XLA Ops:
  0.0 24.3 %all-to-all-start = ((f32[512,1,512]{2,1,0:T(1,128)}), f32[512,1,512]{2,1,0:T(1,128)S(1)}, u32[]{:S(2)}, u32[]{:S(2)}) async-start(f32[512,1,512]{2,1,0:T(1,128)} %bitcast.104), calls=%async_computation | async-start | bytes 2097152 | tf_op jit(solution)/shard_map/all_to_all | solution.py:49
  24.3 4.2 %cosine_multiply_fusion = (f32[512,1,512]{2,0,1:T(8,128)S(1)}, f32[512,1,512]{2,0,1:T(8,128)S(1)}) fusion(s32[512]{0:T(512)S(1)} %get-tuple-element.49), kind=kLoop, calls=%fused_computation.48 | loop fusion | flops 4456448 | bytes 2099200 | tf_op jit(solution)/shard_map/mul | solution.py:56
  28.6 0.2 pad_maximum_fusion
  28.8 2.9 %copy.26 = f32[512,2,512]{2,1,0:T(2,128)} copy(f32[512,2,512]{2,0,1:T(8,128)S(1)} %pad_maximum_fusion) | data formatting | bytes 4194304 | tf_op jit(solution)/shard_map/stack | solution.py:56
  31.7 2.7 %reshape.429 = f32[1024,512]{1,0:T(8,128)S(1)} reshape(f32[512,2,512]{2,1,0:T(2,128)} %copy.26) | data formatting | bytes 4194304 | tf_op jit(solution)/shard_map/reshape | solution.py:56
  34.4 5.9 %fusion.31 = (f32[512,512]{1,0:T(8,128)}, f32[512,512]{1,0:T(8,128)}) fusion(s32[512]{0:T(512)S(1)} %get-tuple-element.50, s32[512]{0:T(512)S(1)} %get-tuple-element.49), kind=kLoop, calls=%fused_computation.55 | loop fusion | flops 3670016 | bytes 2101248 | tf_op jit(solution)/shard_map/sin | solution.py:22
  40.3 42.6 %all-to-all-done = f32[512,1,512]{2,1,0:T(1,128)S(1)} async-done(((f32[512,1,512]{2,1,0:T(1,128)}), f32[512,1,512]{2,1,0:T(1,128)S(1)}, u32[]{:S(2)}, u32[]{:S(2)}) %all-to-all-start) | async-done | bytes 1048608 | tf_op jit(solution)/shard_map/all_to_all | solution.py:49
  82.9 0.1 copy.69
  83.0 4.8 %fusion.89 = f32[1024,512]{1,0:T(8,128)} fusion(f32[1024,512]{1,0:T(8,128)S(1)} %reshape.429, f32[512,512]{1,0:T(8,128)S(1)} %bitcast.97), kind=kOutput, calls=%fused_computation.148 | convolution fusion | flops 3221225472 | bytes 5242880 | tf_op jit(solution)/shard_map/dot_general | solution.py:60
  87.8 2.7 %reshape.430 = f32[512,2,512]{2,1,0:T(2,128)S(1)} reshape(f32[1024,512]{1,0:T(8,128)} %fusion.89) | data formatting | bytes 4194304 | tf_op jit(solution)/shard_map/reshape | solution.py:60
  90.5 0.0 copy-start
  90.5 0.0 copy-start.1
  90.5 1.6 fusion.88
  92.1 0.0 copy-done
  92.1 0.0 copy-done.1
  92.2 0.6 add_bitcast_fusion.1
  92.7 0.7 stack.87
  93.5 1.1 copy.29
  94.6 3.2 %pad_maximum_fusion.1 = f32[512,2,512]{2,1,0:T(2,128)} fusion(f32[512,1,512]{2,1,0:T(1,128)S(1)} %stack.87, f32[512,1,512]{2,1,0:T(1,128)S(1)} %copy.29), kind=kLoop, calls=%fused_computation.1 | loop fusion | flops 524288 | bytes 4194304 | tf_op jit(solution)/shard_map/stack | solution.py:61
  97.8 8.6 %all-to-all-start.1 = ((f32[512,2,512]{2,1,0:T(2,128)}), f32[512,2,512]{2,1,0:T(2,128)S(1)}, u32[]{:S(2)}, u32[]{:S(2)}) async-start(f32[512,2,512]{2,1,0:T(2,128)} %pad_maximum_fusion.1), calls=%async_computation.1 | async-start | bytes 4194304 | tf_op jit(solution)/shard_map/all_to_all | solution.py:62
  106.4 0.1 fusion.70
  106.5 0.1 fusion.68
  106.6 0.1 fusion.67
  106.7 0.1 fusion.62
  106.9 0.8 fusion.60
  107.7 0.3 fusion.56
  107.9 0.6 pad_maximum_fusion.4
  108.6 0.3 fusion.48
  109.0 5.3 %fusion.29 = (f32[32,8192]{1,0:T(8,128)S(1)}, f32[32,8192]{1,0:T(8,128)}) fusion(), kind=kLoop, calls=%fused_computation.53 | loop fusion | flops 3670016 | bytes 2097152 | tf_op jit(solution)/shard_map/sin | solution.py:22
  114.3 93.2 %all-to-all-done.1 = f32[512,2,512]{2,1,0:T(2,128)S(1)} async-done(((f32[512,2,512]{2,1,0:T(2,128)}), f32[512,2,512]{2,1,0:T(2,128)S(1)}, u32[]{:S(2)}, u32[]{:S(2)}) %all-to-all-start.1) | async-done | bytes 2097184 | tf_op jit(solution)/shard_map/all_to_all | solution.py:62
  207.5 3.9 %fusion.9 = f32[2,32,16,512]{3,1,2,0:T(8,128)S(1)} fusion(f32[32,16,2,512]{3,2,1,0:T(2,128)S(1)} %bitcast.96, f32[2,2,32,32]{2,3,1,0:T(8,128)} %pad_maximum_fusion.4), kind=kOutput, calls=%fused_computation.16 | convolution fusion | flops 402653184 | bytes 4210688 | tf_op jit(solution)/shard_map/pqlm,lhqt->pmht/dot_general | solution.py:77
  211.4 0.3 fusion.87
  211.6 0.0 copy-start.2
  211.6 0.1 copy.47
  211.7 0.1 copy.46
  211.8 1.0 copy-done.2
  212.9 0.3 add_bitcast_fusion
  213.1 0.2 copy.49
  213.3 0.2 copy.48
  213.5 0.0 copy-start.3
  213.5 0.0 copy-start.4
  213.5 2.0 fusion.13
  215.6 0.0 copy-done.3
  215.6 0.0 copy-done.4
  215.6 0.4 multiply_add_fusion
  216.0 1.9 fusion.12
  217.9 1.5 copy.34
  (6 shorter events, 0.1 us)
Async XLA Ops:
  0.0 82.9 %all-to-all-start = ((f32[512,1,512]{2,1,0:T(1,128)}), f32[512,1,512]{2,1,0:T(1,128)S(1)}, u32[]{:S(2)}, u32[]{:S(2)}) async-start(f32[512,1,512]{2,1,0:T(1,128)} %bitcast.104), calls=%async_computation | async-start | bytes 2097152 | tf_op jit(solution)/shard_map/all_to_all | solution.py:49
  90.5 1.6 copy-start
  90.5 1.6 copy-start.1
  97.8 109.7 %all-to-all-start.1 = ((f32[512,2,512]{2,1,0:T(2,128)}), f32[512,2,512]{2,1,0:T(2,128)S(1)}, u32[]{:S(2)}, u32[]{:S(2)}) async-start(f32[512,2,512]{2,1,0:T(2,128)} %pad_maximum_fusion.1), calls=%async_computation.1 | async-start | bytes 4194304 | tf_op jit(solution)/shard_map/all_to_all | solution.py:62
  211.6 1.2 copy-start.2
  213.5 2.1 copy-start.3
  213.5 2.1 copy-start.4

commit v4 on v3

--- a/solution.py
+++ b/solution.py
@@ -53,12 +53,12 @@
     frequency = slots // narrow_size + size_a * reversed_digits(slots % narrow_size, levels)
     cosine, sines = unit_turn(frequency[:, None] * slots[None, :] % groups, groups)
     scale = 1.0 / math.sqrt(total_count)
-    table = jnp.stack([cosine * scale, -sines * scale], axis=1).reshape(2 * groups, groups)
+    table = jnp.concatenate([cosine * scale, -sines * scale])
     column_index = here * columns + jnp.arange(columns, dtype=jnp.int32)
     twiddle = unit_turn(frequency[:, None] * column_index[None, :] % total_count, total_count)
     gathered, table, twiddle = lax.optimization_barrier((gathered, table, twiddle))
-    section = jnp.dot(table, gathered, precision=PRECISE).reshape(groups, 2, columns)
-    section = jnp.stack(turn((section[:, 0], section[:, 1]), *twiddle), axis=1)
+    section = jnp.dot(table, gathered, precision=PRECISE).reshape(2, groups, columns)
+    section = jnp.concatenate(turn(section, *twiddle), axis=1)
     owned = lax.all_to_all(section, DEVICES, split_axis=0, concat_axis=0, tiled=True)
 
     index_b = jnp.arange(local_b, dtype=jnp.int32)

time: 220 us -> 218 us (level)
  waiting for transfers between devices: 136 us -> 142 us
  other arithmetic: 22.6 us -> 18.6 us
  local copies, waits for them, and re-layouts: 15.1 us -> 11.9 us
    all_to_all x1, waiting for transfers between devices: 42.6 us -> 49.1 us  [shards(): lax.all_to_all(record.reshape(groups, columns), DEVICES, split_axis=0, co...]
    another operation x3 -> x0, local copies, waits for them, and re-layouts: 4.74 us -> none  [the longest x1 2.94 us: shards(): jnp.stack([cosine * scale, -sines * scale], axis=1)]
    mul x1 -> x0, other arithmetic: 4.25 us -> none  [shards(): cosine * scale]
    another operation x3 -> x0, other arithmetic: 3.96 us -> none  [the longest x2 3.79 us: shards(): section = jnp.stack(turn((section[:, 0], section[:, 1]), *twiddle), axis=1)]
    all_to_all x0 -> x1, local copies, waits for them, and re-layouts: none -> 3.69 us  [shards(): lax.all_to_all(section, DEVICES, split_axis=0, concat_axis=0, tiled=True)]
    sin x6, other arithmetic: 12.5 us -> 15.9 us  [unit_turn(): return (jnp.cos(angles), jnp.sin(angles))]
    reshape x2 -> x1, local copies, waits for them, and re-layouts: 5.4 us -> 3.03 us  [shards(): values = owned.reshape(local_b, groups // local_b, 2, columns)]
  transfers between devices with their start and end apart: 2 -> 2, of which waited for: 2 -> 2; matrix products, arithmetic and copies ran while one was open for 11% -> 8% of each run, Pallas kernels for 0% -> 0%
where the time goes in v4:
time: 218 us; the launch traced here: 217 us
  waiting for transfers between devices  142 us (65%)
  starting transfers between devices  32.9 us (15%)
  other arithmetic  18.6 us (9%)
  local copies, waits for them, and re-layouts  11.9 us (5%)
  matrix products  11.4 us (5%)
    all_to_all x1, waiting for transfers between devices, shards(): lax.all_to_all(section, DEVICES, split_axis=0, concat_axis=0, tiled=True)  93.3 us
    all_to_all x1, waiting for transfers between devices, shards(): lax.all_to_all(record.reshape(groups, columns), DEVICES, split_axis=0, co...  49.1 us
    all_to_all x1, starting transfers between devices, shards(): lax.all_to_all(record.reshape(groups, columns), DEVICES, split_axis=0, co...  24.3 us
    sin x6, other arithmetic, unit_turn(): return (jnp.cos(angles), jnp.sin(angles))  15.9 us
    all_to_all x1, starting transfers between devices, shards(): lax.all_to_all(section, DEVICES, split_axis=0, concat_axis=0, tiled=True)  8.56 us
  transfers between devices with their start and end apart: 2, of which 2 were waited for; matrix products, arithmetic and copies ran while one was open for 8% of the time, Pallas kernels for 0%

profile of v4, /device:TPU:1, one launch (start us, length us, event | category | flops | bytes accessed | tf_op | source)
XLA Modules:
  0.0 217.5 jit_solution(14001259750170833048)
XLA Ops:
  0.0 24.3 %all-to-all-start = ((f32[512,1,512]{2,1,0:T(1,128)}), f32[512,1,512]{2,1,0:T(1,128)S(1)}, u32[]{:S(2)}, u32[]{:S(2)}) async-start(f32[512,1,512]{2,1,0:T(1,128)} %bitcast.94), calls=%async_computation | async-start | bytes 2097152 | tf_op jit(solution)/shard_map/all_to_all | solution.py:49
  24.3 9.4 %fusion.31 = (f32[512,512]{0,1:T(8,128)}, f32[512,512]{0,1:T(8,128)}, f32[512,512]{0,1:T(8,128)S(1)}, f32[512,512]{0,1:T(8,128)S(1)}) fusion(s32[512]{0:T(512)S(1)} %get-tuple-element.48, s32[512]{0:T(512)S(1)} %get-tuple-element.47), kind=kLoop, calls=%fused_computation.54 | loop fusion | flops 8126464 | bytes 4198400 | tf_op jit(solution)/shard_map/sin | solution.py:22
  33.7 0.1 pad_maximum_fusion
  33.9 49.1 %all-to-all-done = f32[512,1,512]{2,1,0:T(1,128)S(1)} async-done(((f32[512,1,512]{2,1,0:T(1,128)}), f32[512,1,512]{2,1,0:T(1,128)S(1)}, u32[]{:S(2)}, u32[]{:S(2)}) %all-to-all-start) | async-done | bytes 1048608 | tf_op jit(solution)/shard_map/all_to_all | solution.py:49
  82.9 0.1 copy.37
  83.0 0.0 copy-start
  83.0 0.0 copy-start.1
  83.0 3.6 %fusion.88 = f32[1024,512]{0,1:T(8,128)S(1)} fusion(f32[1024,512]{0,1:T(8,128)S(1)} %pad_maximum_fusion, f32[512,512]{1,0:T(8,128)S(1)} %bitcast.87), kind=kOutput, calls=%fused_computation.146 | convolution fusion | flops 3221225472 | bytes 5242880 | tf_op jit(solution)/shard_map/dot_general | solution.py:60
  86.7 0.0 copy-done
  86.7 0.0 copy-done.1
  86.7 0.5 multiply_add_fusion.1
  87.2 0.2 maximum_bitcast_fusion
  87.4 3.7 %copy.9 = f32[512,1,1024]{2,1,0:T(1,128)} copy(f32[512,1,1024]{0,2,1:T(8,128)S(1)} %maximum_bitcast_fusion) | data formatting | bytes 4194304 | tf_op jit(solution)/shard_map/all_to_all | solution.py:62
  91.0 8.6 %all-to-all-start.1 = ((f32[512,1,1024]{2,1,0:T(1,128)}), f32[512,1,1024]{2,1,0:T(1,128)S(1)}, u32[]{:S(2)}, u32[]{:S(2)}) async-start(f32[512,1,1024]{2,1,0:T(1,128)} %copy.9), calls=%async_computation.1 | async-start | bytes 4194304 | tf_op jit(solution)/shard_map/all_to_all | solution.py:62
  99.6 0.1 fusion.70
  99.7 0.1 fusion.67
  99.8 0.1 fusion.68
  99.9 0.3 fusion.56
  100.2 0.1 fusion.62
  100.3 0.8 fusion.60
  101.1 0.6 pad_maximum_fusion.3
  101.8 0.3 fusion.48
  102.2 5.3 %fusion.29 = (f32[32,8192]{1,0:T(8,128)S(1)}, f32[32,8192]{1,0:T(8,128)}) fusion(), kind=kLoop, calls=%fused_computation.52 | loop fusion | flops 3670016 | bytes 2097152 | tf_op jit(solution)/shard_map/sin | solution.py:22
  107.4 93.3 %all-to-all-done.1 = f32[512,1,1024]{2,1,0:T(1,128)S(1)} async-done(((f32[512,1,1024]{2,1,0:T(1,128)}), f32[512,1,1024]{2,1,0:T(1,128)S(1)}, u32[]{:S(2)}, u32[]{:S(2)}) %all-to-all-start.1) | async-done | bytes 2097184 | tf_op jit(solution)/shard_map/all_to_all | solution.py:62
  200.7 1.8 copy.36
  202.5 3.0 %reshape.328 = f32[32,16,2,512]{3,2,1,0:T(2,128)S(1)} reshape(f32[512,1024]{1,0:T(8,128)} %bitcast.86) | data formatting | bytes 4194304 | tf_op jit(solution)/shard_map/reshape | solution.py:76
  205.6 3.9 %fusion.9 = f32[2,32,16,512]{3,1,2,0:T(8,128)S(1)} fusion(f32[32,16,2,512]{3,2,1,0:T(2,128)S(1)} %reshape.328, f32[2,2,32,32]{2,3,1,0:T(8,128)} %pad_maximum_fusion.3), kind=kOutput, calls=%fused_computation.17 | convolution fusion | flops 402653184 | bytes 4210688 | tf_op jit(solution)/shard_map/pqlm,lhqt->pmht/dot_general | solution.py:77
  209.5 0.3 fusion.87
  209.7 0.0 copy-start.2
  209.7 0.1 copy.22
  209.8 0.1 copy.23
  209.9 1.0 copy-done.2
  210.9 0.3 add_bitcast_fusion
  211.2 0.2 copy.24
  211.4 0.2 copy.25
  211.6 0.0 copy-start.3
  211.6 0.0 copy-start.4
  211.6 2.0 fusion.13
  213.7 0.0 copy-done.3
  213.7 0.0 copy-done.4
  213.7 0.4 multiply_add_fusion
  214.1 1.9 fusion.12
  216.0 1.5 copy.13
  (6 shorter events, 0.1 us)
Async XLA Ops:
  0.0 82.9 %all-to-all-start = ((f32[512,1,512]{2,1,0:T(1,128)}), f32[512,1,512]{2,1,0:T(1,128)S(1)}, u32[]{:S(2)}, u32[]{:S(2)}) async-start(f32[512,1,512]{2,1,0:T(1,128)} %bitcast.94), calls=%async_computation | async-start | bytes 2097152 | tf_op jit(solution)/shard_map/all_to_all | solution.py:49
  83.0 3.6 %copy-start = (f32[512,512]{0,1:T(8,128)S(1)}, f32[512,512]{0,1:T(8,128)}, u32[]{:S(2)}) copy-start(f32[512,512]{0,1:T(8,128)} %get-tuple-element.20) | copy-start | bytes 3145732
  83.0 3.6 %copy-start.1 = (f32[512,512]{0,1:T(8,128)S(1)}, f32[512,512]{0,1:T(8,128)}, u32[]{:S(2)}) copy-start(f32[512,512]{0,1:T(8,128)} %get-tuple-element.19) | copy-start | bytes 3145732
  91.0 109.7 %all-to-all-start.1 = ((f32[512,1,1024]{2,1,0:T(1,128)}), f32[512,1,1024]{2,1,0:T(1,128)S(1)}, u32[]{:S(2)}, u32[]{:S(2)}) async-start(f32[512,1,1024]{2,1,0:T(1,128)} %copy.9), calls=%async_computation.1 | async-start | bytes 4194304 | tf_op jit(solution)/shard_map/all_to_all | solution.py:62
  209.7 1.2 copy-start.2
  211.6 2.1 copy-start.3
  211.6 2.1 copy-start.4

commit v5 on v4

--- a/solution.py
+++ b/solution.py
@@ -5,7 +5,7 @@
 from jax import lax
 from jax.sharding import PartitionSpec as P
 
-PRECISE = lax.Precision.HIGHEST
+PRECISE = lax.Precision.HIGH
 TWO_PI = 2.0 * math.pi
 DEVICES = ("wide", "narrow")
 

time: 218 us -> 213 us (0.977)
  matrix products: 11.4 us -> 6.97 us
where the time goes in v5:
time: 213 us
  waiting for transfers between devices  142 us (67%)
  starting transfers between devices  32.9 us (15%)
  other arithmetic  18.6 us (9%)
  local copies, waits for them, and re-layouts  11.9 us (6%)
  matrix products  6.97 us (3%)
    all_to_all x1, waiting for transfers between devices, shards(): lax.all_to_all(section, DEVICES, split_axis=0, concat_axis=0, tiled=True)  93.3 us
    all_to_all x1, waiting for transfers between devices, shards(): lax.all_to_all(record.reshape(groups, columns), DEVICES, split_axis=0, co...  49.1 us
    all_to_all x1, starting transfers between devices, shards(): lax.all_to_all(record.reshape(groups, columns), DEVICES, split_axis=0, co...  24.3 us
    sin x6, other arithmetic, unit_turn(): return (jnp.cos(angles), jnp.sin(angles))  15.9 us
    all_to_all x1, starting transfers between devices, shards(): lax.all_to_all(section, DEVICES, split_axis=0, concat_axis=0, tiled=True)  8.56 us
  transfers between devices with their start and end apart: 2, of which 2 were waited for; matrix products, arithmetic and copies ran while one was open for 8% of the time, Pallas kernels for 0%

profile of v5, /device:TPU:1, one launch (start us, length us, event | category | flops | bytes accessed | tf_op | source)
XLA Modules:
  0.0 213.0 jit_solution(14758066005668123531)
XLA Ops:
  0.0 24.3 %all-to-all-start = ((f32[512,1,512]{2,1,0:T(1,128)}), f32[512,1,512]{2,1,0:T(1,128)S(1)}, u32[]{:S(2)}, u32[]{:S(2)}) async-start(f32[512,1,512]{2,1,0:T(1,128)} %bitcast.94), calls=%async_computation | async-start | bytes 2097152 | tf_op jit(solution)/shard_map/all_to_all | solution.py:49
  24.3 9.4 %fusion.31 = (f32[512,512]{0,1:T(8,128)}, f32[512,512]{0,1:T(8,128)}, f32[512,512]{0,1:T(8,128)S(1)}, f32[512,512]{0,1:T(8,128)S(1)}) fusion(s32[512]{0:T(512)S(1)} %get-tuple-element.48, s32[512]{0:T(512)S(1)} %get-tuple-element.47), kind=kLoop, calls=%fused_computation.54 | loop fusion | flops 8126464 | bytes 4198400 | tf_op jit(solution)/shard_map/sin | solution.py:22
  33.7 0.1 pad_maximum_fusion
  33.9 49.1 %all-to-all-done = f32[512,1,512]{2,1,0:T(1,128)S(1)} async-done(((f32[512,1,512]{2,1,0:T(1,128)}), f32[512,1,512]{2,1,0:T(1,128)S(1)}, u32[]{:S(2)}, u32[]{:S(2)}) %all-to-all-start) | async-done | bytes 1048608 | tf_op jit(solution)/shard_map/all_to_all | solution.py:49
  82.9 0.1 copy.37
  83.0 0.0 copy-start
  83.0 0.0 copy-start.1
  83.0 1.9 fusion.88
  84.9 0.0 copy-done
  84.9 0.0 copy-done.1
  84.9 0.5 multiply_add_fusion.1
  85.5 0.2 maximum_bitcast_fusion
  85.6 3.7 %copy.9 = f32[512,1,1024]{2,1,0:T(1,128)} copy(f32[512,1,1024]{0,2,1:T(8,128)S(1)} %maximum_bitcast_fusion) | data formatting | bytes 4194304 | tf_op jit(solution)/shard_map/all_to_all | solution.py:62
  89.3 8.6 %all-to-all-start.1 = ((f32[512,1,1024]{2,1,0:T(1,128)}), f32[512,1,1024]{2,1,0:T(1,128)S(1)}, u32[]{:S(2)}, u32[]{:S(2)}) async-start(f32[512,1,1024]{2,1,0:T(1,128)} %copy.9), calls=%async_computation.1 | async-start | bytes 4194304 | tf_op jit(solution)/shard_map/all_to_all | solution.py:62
  97.9 0.1 fusion.70
  98.0 0.1 fusion.67
  98.1 0.1 fusion.68
  98.2 0.3 fusion.56
  98.5 0.1 fusion.62
  98.6 0.8 fusion.60
  99.4 0.6 pad_maximum_fusion.3
  100.1 0.3 fusion.48
  100.4 5.3 %fusion.29 = (f32[32,8192]{1,0:T(8,128)S(1)}, f32[32,8192]{1,0:T(8,128)}) fusion(), kind=kLoop, calls=%fused_computation.52 | loop fusion | flops 3670016 | bytes 2097152 | tf_op jit(solution)/shard_map/sin | solution.py:22
  105.7 93.3 %all-to-all-done.1 = f32[512,1,1024]{2,1,0:T(1,128)S(1)} async-done(((f32[512,1,1024]{2,1,0:T(1,128)}), f32[512,1,1024]{2,1,0:T(1,128)S(1)}, u32[]{:S(2)}, u32[]{:S(2)}) %all-to-all-start.1) | async-done | bytes 2097184 | tf_op jit(solution)/shard_map/all_to_all | solution.py:62
  199.0 1.8 copy.36
  200.8 3.0 %reshape.328 = f32[32,16,2,512]{3,2,1,0:T(2,128)S(1)} reshape(f32[512,1024]{1,0:T(8,128)} %bitcast.86) | data formatting | bytes 4194304 | tf_op jit(solution)/shard_map/reshape | solution.py:76
  203.8 3.0 %fusion.9 = f32[2,32,16,512]{3,1,2,0:T(8,128)S(1)} fusion(f32[32,16,2,512]{3,2,1,0:T(2,128)S(1)} %reshape.328, f32[2,2,32,32]{2,3,1,0:T(8,128)} %pad_maximum_fusion.3), kind=kOutput, calls=%fused_computation.17 | convolution fusion | flops 201326592 | bytes 4210688 | tf_op jit(solution)/shard_map/pqlm,lhqt->pmht/dot_general | solution.py:77
  206.9 0.3 fusion.87
  207.1 0.0 copy-start.2
  207.1 0.1 copy.22
  207.2 0.1 copy.23
  207.3 1.0 copy-done.2
  208.3 0.3 add_bitcast_fusion
  208.6 0.2 copy.24
  208.8 0.2 copy.25
  209.0 0.0 copy-start.3
  209.0 0.0 copy-start.4
  209.0 1.0 fusion.13
  210.1 0.0 copy-done.3
  210.1 0.0 copy-done.4
  210.1 0.4 multiply_add_fusion
  210.5 1.0 fusion.12
  211.5 1.5 copy.13
  (6 shorter events, 0.1 us)
Async XLA Ops:
  0.0 82.9 %all-to-all-start = ((f32[512,1,512]{2,1,0:T(1,128)}), f32[512,1,512]{2,1,0:T(1,128)S(1)}, u32[]{:S(2)}, u32[]{:S(2)}) async-start(f32[512,1,512]{2,1,0:T(1,128)} %bitcast.94), calls=%async_computation | async-start | bytes 2097152 | tf_op jit(solution)/shard_map/all_to_all | solution.py:49
  83.0 1.9 copy-start
  83.0 1.9 copy-start.1
  89.3 109.7 %all-to-all-start.1 = ((f32[512,1,1024]{2,1,0:T(1,128)}), f32[512,1,1024]{2,1,0:T(1,128)S(1)}, u32[]{:S(2)}, u32[]{:S(2)}) async-start(f32[512,1,1024]{2,1,0:T(1,128)} %copy.9), calls=%async_computation.1 | async-start | bytes 4194304 | tf_op jit(solution)/shard_map/all_to_all | solution.py:62
  207.1 1.2 copy-start.2
  209.0 1.1 copy-start.3
  209.0 1.1 copy-start.4

commit v6 on v5

--- a/solution.py
+++ b/solution.py
@@ -3,11 +3,13 @@
 import jax
 import jax.numpy as jnp
 from jax import lax
+from jax.experimental.layout import Layout, with_layout_constraint
 from jax.sharding import PartitionSpec as P
 
 PRECISE = lax.Precision.HIGH
 TWO_PI = 2.0 * math.pi
 DEVICES = ("wide", "narrow")
+LANES = 128
 
 
 def reversed_digits(number, bit_count):
@@ -57,8 +59,10 @@
     column_index = here * columns + jnp.arange(columns, dtype=jnp.int32)
     twiddle = unit_turn(frequency[:, None] * column_index[None, :] % total_count, total_count)
     gathered, table, twiddle = lax.optimization_barrier((gathered, table, twiddle))
-    section = jnp.dot(table, gathered, precision=PRECISE).reshape(2, groups, columns)
-    section = jnp.concatenate(turn(section, *twiddle), axis=1)
+    section = with_layout_constraint(
+        jnp.dot(table, gathered, precision=PRECISE), Layout(major_to_minor=(0, 1))
+    ).reshape(2, groups, columns)
+    section = jnp.concatenate(turn(section, *twiddle), axis=1).reshape(groups, -1, LANES)
     owned = lax.all_to_all(section, DEVICES, split_axis=0, concat_axis=0, tiled=True)
 
     index_b = jnp.arange(local_b, dtype=jnp.int32)
@@ -73,9 +77,18 @@
     owned, table_b, twiddle_b, table_c, twiddle_c, table_d = lax.optimization_barrier(
         (owned, table_b, twiddle_b, table_c, twiddle_c, table_d)
     )
-    values = owned.reshape(local_b, groups // local_b, 2, columns)
-    values = jnp.einsum("pqlm,lhqt->pmht", table_b, values, precision=PRECISE)
-    values = values.reshape(2, local_b, size_c * size_d)
+    rows = owned.shape[1] // 2
+    values = owned.reshape(local_b, groups // local_b, 2 * rows, LANES)
+    halves = with_layout_constraint(
+        jnp.einsum("pml,lhrc->pmhrc", table_b[0], values, precision=PRECISE),
+        Layout(major_to_minor=(0, 1, 2, 3, 4)),
+    )
+    values = jnp.stack(
+        [
+            halves[0, :, :, :rows] + halves[1, :, :, rows:],
+            halves[0, :, :, rows:] - halves[1, :, :, :rows],
+        ]
+    ).reshape(2, local_b, size_c * size_d)
     values = jnp.stack(turn(values, *twiddle_b)).reshape(2, local_b, size_c, size_d)
     values = jnp.einsum("pqck,qmcd->pmkd", table_c, values, precision=PRECISE)
     values = jnp.stack(turn(values, twiddle_c[0][None], twiddle_c[1][None]))

time: 213 us -> 216 us (1.014)
  other arithmetic: 18.6 us -> 24.6 us
  local copies, waits for them, and re-layouts: 11.9 us -> 8.57 us
    all_to_all x1 -> x0, local copies, waits for them, and re-layouts: 3.69 us -> none  [shards(): lax.all_to_all(section, DEVICES, split_axis=0, concat_axis=0, tiled=True)]
    reshape x1 -> x0, local copies, waits for them, and re-layouts: 3.03 us -> none  [shards(): values = owned.reshape(local_b, groups // local_b, 2, columns)]
    add x0 -> x1, other arithmetic: none -> 2.85 us  [shards(): halves[0, :, :, :rows] + halves[1, :, :, rows:]]
where the time goes in v6:
time: 216 us
  waiting for transfers between devices  142 us (66%)
  starting transfers between devices  32.9 us (15%)
  other arithmetic  24.6 us (11%)
  local copies, waits for them, and re-layouts  8.57 us (4%)
  matrix products  7.6 us (4%)
    all_to_all x1, waiting for transfers between devices, shards(): lax.all_to_all(section, DEVICES, split_axis=0, concat_axis=0, tiled=True)  93.3 us
    all_to_all x1, waiting for transfers between devices, shards(): lax.all_to_all(record.reshape(groups, columns), DEVICES, split_axis=0, co...  48.8 us
    all_to_all x1, starting transfers between devices, shards(): lax.all_to_all(record.reshape(groups, columns), DEVICES, split_axis=0, co...  24.3 us
    sin x6, other arithmetic, unit_turn(): return (jnp.cos(angles), jnp.sin(angles))  16.2 us
    all_to_all x1, starting transfers between devices, shards(): lax.all_to_all(section, DEVICES, split_axis=0, concat_axis=0, tiled=True)  8.56 us
  transfers between devices with their start and end apart: 2, of which 2 were waited for; matrix products, arithmetic and copies ran while one was open for 8% of the time, Pallas kernels for 0%

profile of v6, /device:TPU:1, one launch (start us, length us, event | category | flops | bytes accessed | tf_op | source)
XLA Modules:
  0.0 215.9 jit_solution(8347535646852421941)
XLA Ops:
  0.0 24.3 %all-to-all-start = ((f32[512,1,512]{2,1,0:T(1,128)}), f32[512,1,512]{2,1,0:T(1,128)S(1)}, u32[]{:S(2)}, u32[]{:S(2)}) async-start(f32[512,1,512]{2,1,0:T(1,128)} %bitcast.79), calls=%async_computation | async-start | bytes 2097152 | tf_op jit(solution)/shard_map/all_to_all | solution.py:51
  24.3 9.6 %fusion.28 = (f32[512,512]{1,0:T(8,128)}, f32[512,512]{1,0:T(8,128)}, f32[512,512]{1,0:T(8,128)S(1)}, f32[512,512]{1,0:T(8,128)S(1)}) fusion(s32[512]{0:T(512)S(1)} %get-tuple-element.50, s32[512]{0:T(512)S(1)} %get-tuple-element.49), kind=kLoop, calls=%fused_computation.54 | loop fusion | flops 8126464 | bytes 4198400 | tf_op jit(solution)/shard_map/sin | solution.py:24
  34.0 0.2 pad_maximum_fusion
  34.1 48.8 %all-to-all-done = f32[512,1,512]{2,1,0:T(1,128)S(1)} async-done(((f32[512,1,512]{2,1,0:T(1,128)}), f32[512,1,512]{2,1,0:T(1,128)S(1)}, u32[]{:S(2)}, u32[]{:S(2)}) %all-to-all-start) | async-done | bytes 1048608 | tf_op jit(solution)/shard_map/all_to_all | solution.py:51
  82.9 0.1 copy.32
  83.0 0.0 copy-start
  83.0 0.0 copy-start.1
  83.0 1.9 fusion.86
  84.9 0.0 copy-done
  84.9 0.0 copy-done.1
  84.9 0.6 multiply_add_fusion.1
  85.5 0.2 maximum_bitcast_fusion
  85.7 1.8 copy.20
  87.5 8.6 %all-to-all-start.1 = ((f32[512,8,128]{2,1,0:T(8,128)}), f32[512,8,128]{2,1,0:T(8,128)S(1)}, u32[]{:S(2)}, u32[]{:S(2)}) async-start(f32[512,8,128]{2,1,0:T(8,128)} %bitcast.75), calls=%async_computation.1 | async-start | bytes 4194304 | tf_op jit(solution)/shard_map/all_to_all | solution.py:66
  96.0 0.1 fusion.68
  96.1 0.1 fusion.65
  96.3 0.1 fusion.66
  96.4 0.3 fusion.54
  96.6 0.1 fusion.60
  96.8 0.8 fusion.58
  97.6 0.6 pad_maximum_fusion.3
  98.2 0.3 fusion.46
  98.6 5.3 %fusion.26 = (f32[32,8192]{1,0:T(8,128)S(1)}, f32[32,8192]{1,0:T(8,128)}) fusion(), kind=kLoop, calls=%fused_computation.52 | loop fusion | flops 3670016 | bytes 2097152 | tf_op jit(solution)/shard_map/sin | solution.py:24
  103.8 93.3 %all-to-all-done.1 = f32[512,8,128]{2,1,0:T(8,128)S(1)} async-done(((f32[512,8,128]{2,1,0:T(8,128)}), f32[512,8,128]{2,1,0:T(8,128)S(1)}, u32[]{:S(2)}, u32[]{:S(2)}) %all-to-all-start.1) | async-done | bytes 2097184 | tf_op jit(solution)/shard_map/all_to_all | solution.py:66
  197.2 3.7 %fusion.6 = f32[2,32,16,8,128]{4,1,3,2,0:T(8,128)S(1)} fusion(f32[32,16,8,128]{3,2,1,0:T(8,128)S(1)} %bitcast.74, f32[2,2,32,32]{3,2,1,0:T(8,128)} %pad_maximum_fusion.3), kind=kOutput, calls=%fused_computation.10 | convolution fusion | flops 201326592 | bytes 6324224 | tf_op jit(solution)/shard_map/pml,lhrc->pmhrc/dot_general | solution.py:83
  200.9 2.0 fusion.85
  202.8 1.2 copy_subtract_fusion
  204.1 1.4 sub.41
  205.5 0.0 copy-start.2
  205.5 2.8 %copy_add_fusion = f32[1,32,16,4,128]{4,3,2,1,0:T(4,128)S(1)} fusion(f32[1,32,16,4,128]{4,1,3,2,0:T(8,128)} %get-tuple-element.32, f32[1,32,16,4,128]{4,1,3,2,0:T(8,128)} %get-tuple-element.33), kind=kLoop, calls=%fused_computation.36 | loop fusion | flops 262144 | bytes 3145728 | tf_op jit(solution)/shard_map/add | solution.py:88
  208.3 1.4 add.228
  209.8 0.0 copy-done.2
  209.8 1.8 add_bitcast_fusion
  211.6 0.2 copy.21
  211.8 0.2 copy.22
  211.9 0.0 copy-start.3
  212.0 0.0 copy-start.4
  212.0 1.0 fusion.10
  213.0 0.0 copy-done.3
  213.0 0.0 copy-done.4
  213.0 0.4 multiply_add_fusion
  213.5 1.0 fusion.9
  214.5 1.5 copy.9
  (6 shorter events, 0.1 us)
Async XLA Ops:
  0.0 82.9 %all-to-all-start = ((f32[512,1,512]{2,1,0:T(1,128)}), f32[512,1,512]{2,1,0:T(1,128)S(1)}, u32[]{:S(2)}, u32[]{:S(2)}) async-start(f32[512,1,512]{2,1,0:T(1,128)} %bitcast.79), calls=%async_computation | async-start | bytes 2097152 | tf_op jit(solution)/shard_map/all_to_all | solution.py:51
  83.0 1.9 copy-start
  83.0 1.9 copy-start.1
  87.5 109.7 %all-to-all-start.1 = ((f32[512,8,128]{2,1,0:T(8,128)}), f32[512,8,128]{2,1,0:T(8,128)S(1)}, u32[]{:S(2)}, u32[]{:S(2)}) async-start(f32[512,8,128]{2,1,0:T(8,128)} %bitcast.75), calls=%async_computation.1 | async-start | bytes 4194304 | tf_op jit(solution)/shard_map/all_to_all | solution.py:66
  205.5 4.3 %copy-start.2 = (f32[32,8192]{1,0:T(8,128)S(1)}, f32[32,8192]{1,0:T(8,128)}, u32[]{:S(2)}) copy-start(f32[32,8192]{1,0:T(8,128)} %get-tuple-element.23) | copy-start | bytes 3145732
  211.9 1.1 copy-start.3
  212.0 1.1 copy-start.4

commit v7 on v5

--- a/solution.py
+++ b/solution.py
@@ -3,11 +3,13 @@
 import jax
 import jax.numpy as jnp
 from jax import lax
+from jax.experimental.layout import Layout, with_layout_constraint
 from jax.sharding import PartitionSpec as P
 
 PRECISE = lax.Precision.HIGH
 TWO_PI = 2.0 * math.pi
 DEVICES = ("wide", "narrow")
+LANES = 128
 
 
 def reversed_digits(number, bit_count):
@@ -57,8 +59,10 @@
     column_index = here * columns + jnp.arange(columns, dtype=jnp.int32)
     twiddle = unit_turn(frequency[:, None] * column_index[None, :] % total_count, total_count)
     gathered, table, twiddle = lax.optimization_barrier((gathered, table, twiddle))
-    section = jnp.dot(table, gathered, precision=PRECISE).reshape(2, groups, columns)
-    section = jnp.concatenate(turn(section, *twiddle), axis=1)
+    section = with_layout_constraint(
+        jnp.dot(table, gathered, precision=PRECISE), Layout(major_to_minor=(0, 1))
+    ).reshape(2, groups, columns)
+    section = jnp.concatenate(turn(section, *twiddle), axis=1).reshape(groups, -1, LANES)
     owned = lax.all_to_all(section, DEVICES, split_axis=0, concat_axis=0, tiled=True)
 
     index_b = jnp.arange(local_b, dtype=jnp.int32)

time: 213 us -> 211 us (level)
  local copies, waits for them, and re-layouts: 11.9 us -> 8.66 us
    all_to_all x1 -> x0, local copies, waits for them, and re-layouts: 3.69 us -> none  [shards(): lax.all_to_all(section, DEVICES, split_axis=0, concat_axis=0, tiled=True)]
    unnamed x16 -> x18, local copies, waits for them, and re-layouts: 3.45 us -> 4.96 us
  transfers between devices with their start and end apart: 2 -> 2, of which waited for: 2 -> 2; matrix products, arithmetic and copies ran while one was open for 8% -> 9% of each run, Pallas kernels for 0% -> 0%
where the time goes in v7:
time: 211 us; the launch traced here: 210 us
  waiting for transfers between devices  141 us (67%)
  starting transfers between devices  32.9 us (16%)
  other arithmetic  20 us (9%)
  local copies, waits for them, and re-layouts  8.66 us (4%)
  matrix products  7.65 us (4%)
    all_to_all x1, waiting for transfers between devices, shards(): lax.all_to_all(section, DEVICES, split_axis=0, concat_axis=0, tiled=True)  93.3 us
    all_to_all x1, waiting for transfers between devices, shards(): lax.all_to_all(record.reshape(groups, columns), DEVICES, split_axis=0, co...  47.5 us
    all_to_all x1, starting transfers between devices, shards(): lax.all_to_all(record.reshape(groups, columns), DEVICES, split_axis=0, co...  24.3 us
    sin x6, other arithmetic, unit_turn(): return (jnp.cos(angles), jnp.sin(angles))  16.2 us
    all_to_all x1, starting transfers between devices, shards(): lax.all_to_all(section, DEVICES, split_axis=0, concat_axis=0, tiled=True)  8.56 us
    unnamed x18, local copies, waits for them, and re-layouts  4.96 us
  transfers between devices with their start and end apart: 2, of which 2 were waited for; matrix products, arithmetic and copies ran while one was open for 9% of the time, Pallas kernels for 0%

profile of v7, /device:TPU:1, one launch (start us, length us, event | category | flops | bytes accessed | tf_op | source)
XLA Modules:
  0.0 210.3 jit_solution(2722864491701132291)
XLA Ops:
  0.0 24.3 %all-to-all-start = ((f32[512,1,512]{2,1,0:T(1,128)}), f32[512,1,512]{2,1,0:T(1,128)S(1)}, u32[]{:S(2)}, u32[]{:S(2)}) async-start(f32[512,1,512]{2,1,0:T(1,128)} %bitcast.92), calls=%async_computation | async-start | bytes 2097152 | tf_op jit(solution)/shard_map/all_to_all | solution.py:51
  24.3 9.6 %fusion.31 = (f32[512,512]{1,0:T(8,128)}, f32[512,512]{1,0:T(8,128)}, f32[512,512]{1,0:T(8,128)S(1)}, f32[512,512]{1,0:T(8,128)S(1)}) fusion(s32[512]{0:T(512)S(1)} %get-tuple-element.48, s32[512]{0:T(512)S(1)} %get-tuple-element.47), kind=kLoop, calls=%fused_computation.53 | loop fusion | flops 8126464 | bytes 4198400 | tf_op jit(solution)/shard_map/sin | solution.py:24
  34.0 1.5 pad_maximum_fusion
  35.5 47.5 %all-to-all-done = f32[512,1,512]{2,1,0:T(1,128)S(1)} async-done(((f32[512,1,512]{2,1,0:T(1,128)}), f32[512,1,512]{2,1,0:T(1,128)S(1)}, u32[]{:S(2)}, u32[]{:S(2)}) %all-to-all-start) | async-done | bytes 1048608 | tf_op jit(solution)/shard_map/all_to_all | solution.py:51
  82.9 0.0 copy-start
  82.9 0.1 copy.32
  83.0 1.5 copy-done
  84.5 0.0 copy-start.1
  84.5 0.0 copy-start.2
  84.5 1.8 fusion.88
  86.4 0.0 copy-done.1
  86.4 0.0 copy-done.2
  86.4 0.5 multiply_add_fusion.1
  86.9 0.1 maximum_bitcast_fusion
  87.0 1.8 copy.18
  88.8 8.6 %all-to-all-start.1 = ((f32[512,8,128]{2,1,0:T(8,128)}), f32[512,8,128]{2,1,0:T(8,128)S(1)}, u32[]{:S(2)}, u32[]{:S(2)}) async-start(f32[512,8,128]{2,1,0:T(8,128)} %bitcast.84), calls=%async_computation.1 | async-start | bytes 4194304 | tf_op jit(solution)/shard_map/all_to_all | solution.py:66
  97.4 0.1 fusion.70
  97.5 0.1 fusion.67
  97.6 0.1 fusion.68
  97.7 0.3 fusion.56
  98.0 0.1 fusion.62
  98.1 0.8 fusion.60
  98.9 0.6 pad_maximum_fusion.3
  99.5 0.3 fusion.48
  99.9 5.3 %fusion.29 = (f32[32,8192]{1,0:T(8,128)S(1)}, f32[32,8192]{1,0:T(8,128)}) fusion(), kind=kLoop, calls=%fused_computation.51 | loop fusion | flops 3670016 | bytes 2097152 | tf_op jit(solution)/shard_map/sin | solution.py:24
  105.2 93.3 %all-to-all-done.1 = f32[512,8,128]{2,1,0:T(8,128)S(1)} async-done(((f32[512,8,128]{2,1,0:T(8,128)}), f32[512,8,128]{2,1,0:T(8,128)S(1)}, u32[]{:S(2)}, u32[]{:S(2)}) %all-to-all-start.1) | async-done | bytes 2097184 | tf_op jit(solution)/shard_map/all_to_all | solution.py:66
  198.5 2.1 reshape.330
  200.6 3.8 %fusion.9 = f32[2,32,16,512]{3,1,2,0:T(8,128)S(1)} fusion(f32[32,16,2,512]{3,2,1,0:T(2,128)} %reshape.330, f32[2,2,32,32]{2,3,1,0:T(8,128)} %pad_maximum_fusion.3), kind=kOutput, calls=%fused_computation.16 | convolution fusion | flops 201326592 | bytes 4210688 | tf_op jit(solution)/shard_map/pqlm,lhqt->pmht/dot_general | solution.py:81
  204.3 0.2 fusion.87
  204.5 0.0 copy-start.3
  204.6 0.1 copy.19
  204.6 0.1 copy.20
  204.7 1.0 copy-done.3
  205.8 0.3 add_bitcast_fusion
  206.0 0.2 copy.21
  206.2 0.2 copy.22
  206.4 0.0 copy-start.4
  206.4 0.0 copy-start.5
  206.4 1.0 fusion.13
  207.5 0.0 copy-done.4
  207.5 0.0 copy-done.5
  207.5 0.3 multiply_add_fusion
  207.8 1.0 fusion.12
  208.8 1.5 copy.10
  (6 shorter events, 0.1 us)
Async XLA Ops:
  0.0 82.9 %all-to-all-start = ((f32[512,1,512]{2,1,0:T(1,128)}), f32[512,1,512]{2,1,0:T(1,128)S(1)}, u32[]{:S(2)}, u32[]{:S(2)}) async-start(f32[512,1,512]{2,1,0:T(1,128)} %bitcast.92), calls=%async_computation | async-start | bytes 2097152 | tf_op jit(solution)/shard_map/all_to_all | solution.py:51
  82.9 1.6 copy-start
  84.5 1.8 copy-start.1
  84.5 1.9 copy-start.2
  88.8 109.7 %all-to-all-start.1 = ((f32[512,8,128]{2,1,0:T(8,128)}), f32[512,8,128]{2,1,0:T(8,128)S(1)}, u32[]{:S(2)}, u32[]{:S(2)}) async-start(f32[512,8,128]{2,1,0:T(8,128)} %bitcast.84), calls=%async_computation.1 | async-start | bytes 4194304 | tf_op jit(solution)/shard_map/all_to_all | solution.py:66
  204.5 1.2 copy-start.3
  206.4 1.1 copy-start.4
  206.4 1.1 copy-start.5

commit v8 on v7

--- a/solution.py
+++ b/solution.py
@@ -83,7 +83,8 @@
     values = jnp.stack(turn(values, *twiddle_b)).reshape(2, local_b, size_c, size_d)
     values = jnp.einsum("pqck,qmcd->pmkd", table_c, values, precision=PRECISE)
     values = jnp.stack(turn(values, twiddle_c[0][None], twiddle_c[1][None]))
-    values = jnp.einsum("pqdk,qmcd->pmck", table_d, values, precision=PRECISE)
+    values = jnp.broadcast_to(values.reshape(1, 2, local_b * size_c, size_d), (2,) + values.shape[:1] + (local_b * size_c, size_d))
+    values = jnp.einsum("pqdk,pqnd->pnk", table_d, values, precision=PRECISE)
     return values.reshape(2, 1, 1, local_b, size_c, size_d)
 
 

time: 211 us -> 210 us (level)
  local copies, waits for them, and re-layouts: 8.66 us -> 5.78 us
  matrix products: 7.65 us -> 9.8 us
    dot_general x1, matrix products: 1.01 us -> 3.12 us  [shards(): values = jnp.einsum('pqdk,pqnd->pnk', table_d, values, precision=PRECISE)]
    unnamed x18 -> x16, local copies, waits for them, and re-layouts: 4.96 us -> 3.45 us
  transfers between devices with their start and end apart: 2 -> 2, of which waited for: 2 -> 2; matrix products, arithmetic and copies ran while one was open for 9% -> 8% of each run, Pallas kernels for 0% -> 0%
where the time goes in v8:
time: 210 us
  waiting for transfers between devices  142 us (68%)
  starting transfers between devices  32.9 us (16%)
  other arithmetic  19.2 us (9%)
  matrix products  9.8 us (5%)
  local copies, waits for them, and re-layouts  5.78 us (3%)
    all_to_all x1, waiting for transfers between devices, shards(): lax.all_to_all(section, DEVICES, split_axis=0, concat_axis=0, tiled=True)  93.3 us
    all_to_all x1, waiting for transfers between devices, shards(): lax.all_to_all(record.reshape(groups, columns), DEVICES, split_axis=0, co...  48.8 us
    all_to_all x1, starting transfers between devices, shards(): lax.all_to_all(record.reshape(groups, columns), DEVICES, split_axis=0, co...  24.3 us
    sin x6, other arithmetic, unit_turn(): return (jnp.cos(angles), jnp.sin(angles))  16.2 us
    all_to_all x1, starting transfers between devices, shards(): lax.all_to_all(section, DEVICES, split_axis=0, concat_axis=0, tiled=True)  8.56 us
  transfers between devices with their start and end apart: 2, of which 2 were waited for; matrix products, arithmetic and copies ran while one was open for 8% of the time, Pallas kernels for 0%

profile of v8, /device:TPU:1, one launch (start us, length us, event | category | flops | bytes accessed | tf_op | source)
XLA Modules:
  0.0 210.0 jit_solution(9399954552277403280)
XLA Ops:
  0.0 24.3 %all-to-all-start = ((f32[512,1,512]{2,1,0:T(1,128)}), f32[512,1,512]{2,1,0:T(1,128)S(1)}, u32[]{:S(2)}, u32[]{:S(2)}) async-start(f32[512,1,512]{2,1,0:T(1,128)} %bitcast.88), calls=%async_computation | async-start | bytes 2097152 | tf_op jit(solution)/shard_map/all_to_all | solution.py:51
  24.3 9.6 %fusion.29 = (f32[512,512]{1,0:T(8,128)}, f32[512,512]{1,0:T(8,128)}, f32[512,512]{1,0:T(8,128)S(1)}, f32[512,512]{1,0:T(8,128)S(1)}) fusion(s32[512]{0:T(512)S(1)} %get-tuple-element.48, s32[512]{0:T(512)S(1)} %get-tuple-element.47), kind=kLoop, calls=%fused_computation.51 | loop fusion | flops 8126464 | bytes 4198400 | tf_op jit(solution)/shard_map/sin | solution.py:24
  34.0 0.2 pad_maximum_fusion
  34.1 48.8 %all-to-all-done = f32[512,1,512]{2,1,0:T(1,128)S(1)} async-done(((f32[512,1,512]{2,1,0:T(1,128)}), f32[512,1,512]{2,1,0:T(1,128)S(1)}, u32[]{:S(2)}, u32[]{:S(2)}) %all-to-all-start) | async-done | bytes 1048608 | tf_op jit(solution)/shard_map/all_to_all | solution.py:51
  82.9 0.1 copy.31
  83.0 0.0 copy-start
  83.0 0.0 copy-start.1
  83.0 1.9 fusion.84
  84.9 0.0 copy-done
  84.9 0.0 copy-done.1
  84.9 0.6 multiply_add_fusion.1
  85.5 0.2 maximum_bitcast_fusion
  85.7 1.8 copy.17
  87.5 8.6 %all-to-all-start.1 = ((f32[512,8,128]{2,1,0:T(8,128)}), f32[512,8,128]{2,1,0:T(8,128)S(1)}, u32[]{:S(2)}, u32[]{:S(2)}) async-start(f32[512,8,128]{2,1,0:T(8,128)} %bitcast.78), calls=%async_computation.1 | async-start | bytes 4194304 | tf_op jit(solution)/shard_map/all_to_all | solution.py:66
  96.0 0.1 fusion.67
  96.1 0.1 fusion.64
  96.3 0.1 fusion.65
  96.4 0.3 fusion.53
  96.6 0.1 fusion.59
  96.8 0.8 fusion.57
  97.6 0.6 pad_maximum_fusion.3
  98.2 0.3 fusion.45
  98.6 5.3 %fusion.27 = (f32[32,8192]{1,0:T(8,128)S(1)}, f32[32,8192]{1,0:T(8,128)}) fusion(), kind=kLoop, calls=%fused_computation.49 | loop fusion | flops 3670016 | bytes 2097152 | tf_op jit(solution)/shard_map/sin | solution.py:24
  103.9 93.3 %all-to-all-done.1 = f32[512,8,128]{2,1,0:T(8,128)S(1)} async-done(((f32[512,8,128]{2,1,0:T(8,128)}), f32[512,8,128]{2,1,0:T(8,128)S(1)}, u32[]{:S(2)}, u32[]{:S(2)}) %all-to-all-start.1) | async-done | bytes 2097184 | tf_op jit(solution)/shard_map/all_to_all | solution.py:66
  197.2 2.1 reshape.333
  199.2 3.8 %fusion.8 = f32[2,32,16,512]{3,1,2,0:T(8,128)S(1)} fusion(f32[32,16,2,512]{3,2,1,0:T(2,128)} %reshape.333, f32[2,2,32,32]{2,3,1,0:T(8,128)} %pad_maximum_fusion.3), kind=kOutput, calls=%fused_computation.15 | convolution fusion | flops 201326592 | bytes 4210688 | tf_op jit(solution)/shard_map/pqlm,lhqt->pmht/dot_general | solution.py:81
  203.0 0.3 fusion.83
  203.3 0.0 copy-start.2
  203.3 0.1 copy.18
  203.4 0.1 copy.19
  203.5 1.0 copy-done.2
  204.5 0.3 add_bitcast_fusion
  204.8 0.2 copy.20
  205.0 0.2 copy.21
  205.2 0.0 copy-start.3
  205.2 0.0 copy-start.4
  205.2 1.0 fusion.11
  206.2 0.0 copy-done.3
  206.2 0.0 copy-done.4
  206.2 0.4 multiply_add_fusion
  206.7 0.1 maximum_bitcast_fusion.3
  206.8 3.1 %fusion.6 = f32[2,2048,128,1]{2,1,3,0:T(8,128)} fusion(f32[2,2,128,128]{3,2,1,0:T(8,128)S(1)} %pad_maximum_fusion.1, f32[2,2048,128]{2,1,0:T(8,128)S(1)} %maximum_bitcast_fusion.3), kind=kOutput, calls=%fused_computation.10 | convolution fusion | flops 805306368 | bytes 4456448 | tf_op jit(solution)/shard_map/pqdk,pqnd->pnk/dot_general | solution.py:87
  (6 shorter events, 0.1 us)
Async XLA Ops:
  0.0 82.9 %all-to-all-start = ((f32[512,1,512]{2,1,0:T(1,128)}), f32[512,1,512]{2,1,0:T(1,128)S(1)}, u32[]{:S(2)}, u32[]{:S(2)}) async-start(f32[512,1,512]{2,1,0:T(1,128)} %bitcast.88), calls=%async_computation | async-start | bytes 2097152 | tf_op jit(solution)/shard_map/all_to_all | solution.py:51
  83.0 1.9 copy-start
  83.0 1.9 copy-start.1
  87.5 109.7 %all-to-all-start.1 = ((f32[512,8,128]{2,1,0:T(8,128)}), f32[512,8,128]{2,1,0:T(8,128)S(1)}, u32[]{:S(2)}, u32[]{:S(2)}) async-start(f32[512,8,128]{2,1,0:T(8,128)} %bitcast.78), calls=%async_computation.1 | async-start | bytes 4194304 | tf_op jit(solution)/shard_map/all_to_all | solution.py:66
  203.3 1.2 copy-start.2
  205.2 1.1 copy-start.3
  205.2 1.1 copy-start.4

commit v9 on v7

--- a/solution.py
+++ b/solution.py
@@ -62,7 +62,9 @@
     section = with_layout_constraint(
         jnp.dot(table, gathered, precision=PRECISE), Layout(major_to_minor=(0, 1))
     ).reshape(2, groups, columns)
-    section = jnp.concatenate(turn(section, *twiddle), axis=1).reshape(groups, -1, LANES)
+    section = with_layout_constraint(
+        jnp.stack(turn(section, *twiddle), axis=1), Layout((0, 1, 2))
+    )
     owned = lax.all_to_all(section, DEVICES, split_axis=0, concat_axis=0, tiled=True)
 
     index_b = jnp.arange(local_b, dtype=jnp.int32)

time: 211 us -> 210 us (level)
  local copies, waits for them, and re-layouts: 8.66 us -> 5.19 us
    another operation x0 -> x2, other arithmetic: none -> 3.7 us  [shards(): jnp.stack(turn(section, *twiddle), axis=1)]
    unnamed x18 -> x15, local copies, waits for them, and re-layouts: 4.96 us -> 1.67 us
  transfers between devices with their start and end apart: 2 -> 2, of which waited for: 2 -> 2; matrix products, arithmetic and copies ran while one was open for 9% -> 8% of each run, Pallas kernels for 0% -> 0%
where the time goes in v9:
time: 210 us; the launch traced here: 209 us
  waiting for transfers between devices  142 us (68%)
  starting transfers between devices  32.9 us (16%)
  other arithmetic  22 us (10%)
  matrix products  6.94 us (3%)
  local copies, waits for them, and re-layouts  5.19 us (2%)
    all_to_all x1, waiting for transfers between devices, shards(): lax.all_to_all(section, DEVICES, split_axis=0, concat_axis=0, tiled=True)  93.5 us
    all_to_all x1, waiting for transfers between devices, shards(): lax.all_to_all(record.reshape(groups, columns), DEVICES, split_axis=0, co...  48.8 us
    all_to_all x1, starting transfers between devices, shards(): lax.all_to_all(record.reshape(groups, columns), DEVICES, split_axis=0, co...  24.3 us
    sin x6, other arithmetic, unit_turn(): return (jnp.cos(angles), jnp.sin(angles))  16.2 us
    all_to_all x1, starting transfers between devices, shards(): lax.all_to_all(section, DEVICES, split_axis=0, concat_axis=0, tiled=True)  8.56 us
  transfers between devices with their start and end apart: 2, of which 2 were waited for; matrix products, arithmetic and copies ran while one was open for 8% of the time, Pallas kernels for 0%

profile of v9, /device:TPU:1, one launch (start us, length us, event | category | flops | bytes accessed | tf_op | source)
XLA Modules:
  0.0 209.5 jit_solution(11924681907002369864)
XLA Ops:
  0.0 24.3 %all-to-all-start = ((f32[512,1,512]{2,1,0:T(1,128)}), f32[512,1,512]{2,1,0:T(1,128)S(1)}, u32[]{:S(2)}, u32[]{:S(2)}) async-start(f32[512,1,512]{2,1,0:T(1,128)} %bitcast.92), calls=%async_computation | async-start | bytes 2097152 | tf_op jit(solution)/shard_map/all_to_all | solution.py:51
  24.3 9.6 %fusion.31 = (f32[512,512]{1,0:T(8,128)}, f32[512,512]{1,0:T(8,128)}, f32[512,512]{1,0:T(8,128)S(1)}, f32[512,512]{1,0:T(8,128)S(1)}) fusion(s32[512]{0:T(512)S(1)} %get-tuple-element.48, s32[512]{0:T(512)S(1)} %get-tuple-element.47), kind=kLoop, calls=%fused_computation.53 | loop fusion | flops 8126464 | bytes 4198400 | tf_op jit(solution)/shard_map/sin | solution.py:24
  34.0 0.2 pad_maximum_fusion
  34.1 48.8 %all-to-all-done = f32[512,1,512]{2,1,0:T(1,128)S(1)} async-done(((f32[512,1,512]{2,1,0:T(1,128)}), f32[512,1,512]{2,1,0:T(1,128)S(1)}, u32[]{:S(2)}, u32[]{:S(2)}) %all-to-all-start) | async-done | bytes 1048608 | tf_op jit(solution)/shard_map/all_to_all | solution.py:51
  82.9 0.1 copy.35
  83.0 0.0 copy-start
  83.0 0.0 copy-start.1
  83.0 1.9 fusion.88
  84.9 0.0 copy-done
  84.9 0.0 copy-done.1
  84.9 0.5 add_bitcast_fusion.1
  85.4 1.1 copy.10
  86.5 0.7 stack.81
  87.2 3.2 %pad_maximum_fusion.1 = f32[512,2,512]{2,1,0:T(2,128)} fusion(f32[512,1,512]{2,1,0:T(1,128)S(1)} %stack.81, f32[512,1,512]{2,1,0:T(1,128)S(1)} %copy.10), kind=kLoop, calls=%fused_computation.1 | loop fusion | flops 524288 | bytes 4194304 | tf_op jit(solution)/shard_map/stack | solution.py:66
  90.4 8.6 %all-to-all-start.1 = ((f32[512,2,512]{2,1,0:T(2,128)}), f32[512,2,512]{2,1,0:T(2,128)S(1)}, u32[]{:S(2)}, u32[]{:S(2)}) async-start(f32[512,2,512]{2,1,0:T(2,128)} %pad_maximum_fusion.1), calls=%async_computation.1 | async-start | bytes 4194304 | tf_op jit(solution)/shard_map/all_to_all | solution.py:68
  99.0 0.1 fusion.70
  99.1 0.1 fusion.67
  99.2 0.1 fusion.68
  99.3 0.3 fusion.56
  99.6 0.1 fusion.62
  99.7 0.8 fusion.60
  100.5 0.6 pad_maximum_fusion.4
  101.2 0.3 fusion.48
  101.5 5.3 %fusion.29 = (f32[32,8192]{1,0:T(8,128)S(1)}, f32[32,8192]{1,0:T(8,128)}) fusion(), kind=kLoop, calls=%fused_computation.51 | loop fusion | flops 3670016 | bytes 2097152 | tf_op jit(solution)/shard_map/sin | solution.py:24
  106.8 93.5 %all-to-all-done.1 = f32[512,2,512]{2,1,0:T(2,128)S(1)} async-done(((f32[512,2,512]{2,1,0:T(2,128)}), f32[512,2,512]{2,1,0:T(2,128)S(1)}, u32[]{:S(2)}, u32[]{:S(2)}) %all-to-all-start.1) | async-done | bytes 2097184 | tf_op jit(solution)/shard_map/all_to_all | solution.py:68
  200.3 3.0 %fusion.9 = f32[2,32,16,512]{3,1,2,0:T(8,128)S(1)} fusion(f32[32,16,2,512]{3,2,1,0:T(2,128)S(1)} %bitcast.84, f32[2,2,32,32]{2,3,1,0:T(8,128)} %pad_maximum_fusion.4), kind=kOutput, calls=%fused_computation.16 | convolution fusion | flops 201326592 | bytes 4210688 | tf_op jit(solution)/shard_map/pqlm,lhqt->pmht/dot_general | solution.py:83
  203.3 0.3 fusion.87
  203.6 0.0 copy-start.2
  203.6 0.1 copy.22
  203.7 0.1 copy.23
  203.8 1.0 copy-done.2
  204.8 0.3 add_bitcast_fusion
  205.1 0.2 copy.24
  205.3 0.2 copy.25
  205.5 0.0 copy-start.3
  205.5 0.0 copy-start.4
  205.5 1.0 fusion.13
  206.6 0.0 copy-done.3
  206.6 0.0 copy-done.4
  206.6 0.4 multiply_add_fusion
  207.0 1.0 fusion.12
  208.0 1.5 copy.14
  (6 shorter events, 0.1 us)
Async XLA Ops:
  0.0 82.9 %all-to-all-start = ((f32[512,1,512]{2,1,0:T(1,128)}), f32[512,1,512]{2,1,0:T(1,128)S(1)}, u32[]{:S(2)}, u32[]{:S(2)}) async-start(f32[512,1,512]{2,1,0:T(1,128)} %bitcast.92), calls=%async_computation | async-start | bytes 2097152 | tf_op jit(solution)/shard_map/all_to_all | solution.py:51
  83.0 1.9 copy-start
  83.0 1.9 copy-start.1
  90.4 109.9 %all-to-all-start.1 = ((f32[512,2,512]{2,1,0:T(2,128)}), f32[512,2,512]{2,1,0:T(2,128)S(1)}, u32[]{:S(2)}, u32[]{:S(2)}) async-start(f32[512,2,512]{2,1,0:T(2,128)} %pad_maximum_fusion.1), calls=%async_computation.1 | async-start | bytes 4194304 | tf_op jit(solution)/shard_map/all_to_all | solution.py:68
  203.6 1.2 copy-start.2
  205.5 1.1 copy-start.3
  205.5 1.1 copy-start.4

commit v10 on v7

--- a/solution.py
+++ b/solution.py
@@ -62,7 +62,9 @@
     section = with_layout_constraint(
         jnp.dot(table, gathered, precision=PRECISE), Layout(major_to_minor=(0, 1))
     ).reshape(2, groups, columns)
-    section = jnp.concatenate(turn(section, *twiddle), axis=1).reshape(groups, -1, LANES)
+    real, imag = (part[:, None] for part in turn(section, *twiddle))
+    part_index = lax.broadcasted_iota(jnp.int32, (groups, 2, columns), 1)
+    section = with_layout_constraint(jnp.where(part_index == 0, real, imag), Layout((0, 1, 2)))
     owned = lax.all_to_all(section, DEVICES, split_axis=0, concat_axis=0, tiled=True)
 
     index_b = jnp.arange(local_b, dtype=jnp.int32)

time: 211 us -> 207 us (0.981)
  local copies, waits for them, and re-layouts: 8.66 us -> 3.39 us
    unnamed x18 -> x15, local copies, waits for them, and re-layouts: 4.96 us -> 1.67 us
    select_n x0 -> x1, other arithmetic: none -> 2.2 us  [shards(): jnp.where(part_index == 0, real, imag)]
where the time goes in v10:
time: 207 us; the launch traced here: 206 us
  waiting for transfers between devices  142 us (69%)
  starting transfers between devices  32.9 us (16%)
  other arithmetic  21 us (10%)
  matrix products  6.93 us (3%)
  local copies, waits for them, and re-layouts  3.39 us (2%)
    all_to_all x1, waiting for transfers between devices, shards(): lax.all_to_all(section, DEVICES, split_axis=0, concat_axis=0, tiled=True)  93.3 us
    all_to_all x1, waiting for transfers between devices, shards(): lax.all_to_all(record.reshape(groups, columns), DEVICES, split_axis=0, co...  48.8 us
    all_to_all x1, starting transfers between devices, shards(): lax.all_to_all(record.reshape(groups, columns), DEVICES, split_axis=0, co...  24.3 us
    sin x6, other arithmetic, unit_turn(): return (jnp.cos(angles), jnp.sin(angles))  16.2 us
    all_to_all x1, starting transfers between devices, shards(): lax.all_to_all(section, DEVICES, split_axis=0, concat_axis=0, tiled=True)  8.56 us
  transfers between devices with their start and end apart: 2, of which 2 were waited for; matrix products, arithmetic and copies ran while one was open for 9% of the time, Pallas kernels for 0%

profile of v10, /device:TPU:1, one launch (start us, length us, event | category | flops | bytes accessed | tf_op | source)
XLA Modules:
  0.0 206.5 jit_solution(2383980125755751319)
XLA Ops:
  0.0 24.3 %all-to-all-start = ((f32[512,1,512]{2,1,0:T(1,128)}), f32[512,1,512]{2,1,0:T(1,128)S(1)}, u32[]{:S(2)}, u32[]{:S(2)}) async-start(f32[512,1,512]{2,1,0:T(1,128)} %bitcast.90), calls=%async_computation | async-start | bytes 2097152 | tf_op jit(solution)/shard_map/all_to_all | solution.py:51
  24.4 9.6 %fusion.31 = (f32[512,512]{1,0:T(8,128)}, f32[512,512]{1,0:T(8,128)}, f32[512,512]{1,0:T(8,128)S(1)}, f32[512,512]{1,0:T(8,128)S(1)}) fusion(s32[512]{0:T(512)S(1)} %get-tuple-element.48, s32[512]{0:T(512)S(1)} %get-tuple-element.47), kind=kLoop, calls=%fused_computation.53 | loop fusion | flops 8126464 | bytes 4198400 | tf_op jit(solution)/shard_map/sin | solution.py:24
  34.0 0.2 pad_maximum_fusion
  34.2 48.8 %all-to-all-done = f32[512,1,512]{2,1,0:T(1,128)S(1)} async-done(((f32[512,1,512]{2,1,0:T(1,128)}), f32[512,1,512]{2,1,0:T(1,128)S(1)}, u32[]{:S(2)}, u32[]{:S(2)}) %all-to-all-start) | async-done | bytes 1048608 | tf_op jit(solution)/shard_map/all_to_all | solution.py:51
  82.9 0.1 copy.32
  83.0 0.0 copy-start
  83.0 0.0 copy-start.1
  83.0 1.9 fusion.88
  84.9 0.0 copy-done
  84.9 0.0 copy-done.1
  84.9 0.5 multiply_add_fusion.1
  85.4 2.2 %broadcast_select_fusion = f32[512,2,512]{2,1,0:T(2,128)} fusion(pred[2]{0:T(512)(128)(4,1)S(1)} %iota_compare_fusion, f32[512,512]{1,0:T(8,128)S(1)} %get-tuple-element.32, f32[512,512]{1,0:T(8,128)S(1)} %get-tuple-element.31), kind=kLoop, calls=%fused_computation.12 | loop fusion | flops 524288 | bytes 4194306 | tf_op jit(solution)/shard_map/jit(_where)/select_n | solution.py:67
  87.6 8.6 %all-to-all-start.1 = ((f32[512,2,512]{2,1,0:T(2,128)}), f32[512,2,512]{2,1,0:T(2,128)S(1)}, u32[]{:S(2)}, u32[]{:S(2)}) async-start(f32[512,2,512]{2,1,0:T(2,128)} %broadcast_select_fusion), calls=%async_computation.1 | async-start | bytes 4194304 | tf_op jit(solution)/shard_map/all_to_all | solution.py:68
  96.2 0.1 fusion.70
  96.3 0.1 fusion.67
  96.4 0.1 fusion.68
  96.5 0.3 fusion.56
  96.8 0.1 fusion.62
  96.9 0.8 fusion.60
  97.7 0.6 pad_maximum_fusion.3
  98.3 0.3 fusion.48
  98.7 5.3 %fusion.29 = (f32[32,8192]{1,0:T(8,128)S(1)}, f32[32,8192]{1,0:T(8,128)}) fusion(), kind=kLoop, calls=%fused_computation.51 | loop fusion | flops 3670016 | bytes 2097152 | tf_op jit(solution)/shard_map/sin | solution.py:24
  104.0 93.3 %all-to-all-done.1 = f32[512,2,512]{2,1,0:T(2,128)S(1)} async-done(((f32[512,2,512]{2,1,0:T(2,128)}), f32[512,2,512]{2,1,0:T(2,128)S(1)}, u32[]{:S(2)}, u32[]{:S(2)}) %all-to-all-start.1) | async-done | bytes 2097184 | tf_op jit(solution)/shard_map/all_to_all | solution.py:68
  197.3 3.0 %fusion.9 = f32[2,32,16,512]{3,1,2,0:T(8,128)S(1)} fusion(f32[32,16,2,512]{3,2,1,0:T(2,128)S(1)} %bitcast.82, f32[2,2,32,32]{2,3,1,0:T(8,128)} %pad_maximum_fusion.3), kind=kOutput, calls=%fused_computation.16 | convolution fusion | flops 201326592 | bytes 4210688 | tf_op jit(solution)/shard_map/pqlm,lhqt->pmht/dot_general | solution.py:83
  200.3 0.3 fusion.87
  200.6 0.0 copy-start.2
  200.6 0.1 copy.19
  200.7 0.1 copy.20
  200.8 1.0 copy-done.2
  201.8 0.3 add_bitcast_fusion
  202.1 0.2 copy.21
  202.3 0.2 copy.22
  202.5 0.0 copy-start.3
  202.5 0.0 copy-start.4
  202.5 1.0 fusion.13
  203.6 0.0 copy-done.3
  203.6 0.0 copy-done.4
  203.6 0.4 multiply_add_fusion
  204.0 1.0 fusion.12
  205.0 1.5 copy.11
  (7 shorter events, 0.1 us)
Async XLA Ops:
  0.0 82.9 %all-to-all-start = ((f32[512,1,512]{2,1,0:T(1,128)}), f32[512,1,512]{2,1,0:T(1,128)S(1)}, u32[]{:S(2)}, u32[]{:S(2)}) async-start(f32[512,1,512]{2,1,0:T(1,128)} %bitcast.90), calls=%async_computation | async-start | bytes 2097152 | tf_op jit(solution)/shard_map/all_to_all | solution.py:51
  83.0 1.9 copy-start
  83.0 1.9 copy-start.1
  87.6 109.7 %all-to-all-start.1 = ((f32[512,2,512]{2,1,0:T(2,128)}), f32[512,2,512]{2,1,0:T(2,128)S(1)}, u32[]{:S(2)}, u32[]{:S(2)}) async-start(f32[512,2,512]{2,1,0:T(2,128)} %broadcast_select_fusion), calls=%async_computation.1 | async-start | bytes 4194304 | tf_op jit(solution)/shard_map/all_to_all | solution.py:68
  200.6 1.2 copy-start.2
  202.5 1.1 copy-start.3
  202.5 1.1 copy-start.4

commit v11 on v7

--- a/solution.py
+++ b/solution.py
@@ -62,7 +62,11 @@
     section = with_layout_constraint(
         jnp.dot(table, gathered, precision=PRECISE), Layout(major_to_minor=(0, 1))
     ).reshape(2, groups, columns)
-    section = jnp.concatenate(turn(section, *twiddle), axis=1).reshape(groups, -1, LANES)
+    first = lax.broadcasted_iota(jnp.int32, (groups, 2, columns), 1) == 0
+    real, imag = section[0][:, None], section[1][:, None]
+    cosine, sines = twiddle[0][:, None], twiddle[1][:, None]
+    section = jnp.where(first, real, imag) * cosine + jnp.where(first, imag, -real) * sines
+    section = with_layout_constraint(section, Layout((0, 1, 2)))
     owned = lax.all_to_all(section, DEVICES, split_axis=0, concat_axis=0, tiled=True)
 
     index_b = jnp.arange(local_b, dtype=jnp.int32)

time: 211 us -> 213 us (level)
  other arithmetic: 20 us -> 26.4 us
  local copies, waits for them, and re-layouts: 8.66 us -> 4.5 us
    add x0 -> x1, other arithmetic: none -> 7.7 us  [shards(): jnp.where(first, real, imag) * cosine]
    unnamed x18 -> x15, local copies, waits for them, and re-layouts: 4.96 us -> 2.77 us
  transfers between devices with their start and end apart: 2 -> 2, of which waited for: 2 -> 2; matrix products, arithmetic and copies ran while one was open for 9% -> 8% of each run, Pallas kernels for 0% -> 0%
where the time goes in v11:
time: 213 us
  waiting for transfers between devices  142 us (67%)
  starting transfers between devices  32.9 us (15%)
  other arithmetic  26.4 us (12%)
  matrix products  6.94 us (3%)
  local copies, waits for them, and re-layouts  4.5 us (2%)
    all_to_all x1, waiting for transfers between devices, shards(): lax.all_to_all(section, DEVICES, split_axis=0, concat_axis=0, tiled=True)  93.3 us
    all_to_all x1, waiting for transfers between devices, shards(): lax.all_to_all(record.reshape(groups, columns), DEVICES, split_axis=0, co...  48.8 us
    all_to_all x1, starting transfers between devices, shards(): lax.all_to_all(record.reshape(groups, columns), DEVICES, split_axis=0, co...  24.3 us
    sin x6, other arithmetic, unit_turn(): return (jnp.cos(angles), jnp.sin(angles))  16.2 us
    all_to_all x1, starting transfers between devices, shards(): lax.all_to_all(section, DEVICES, split_axis=0, concat_axis=0, tiled=True)  8.56 us
    add x1, other arithmetic, shards(): jnp.where(first, real, imag) * cosine  7.7 us
  transfers between devices with their start and end apart: 2, of which 2 were waited for; matrix products, arithmetic and copies ran while one was open for 8% of the time, Pallas kernels for 0%

profile of v11, /device:TPU:1, one launch (start us, length us, event | category | flops | bytes accessed | tf_op | source)
XLA Modules:
  0.0 213.0 jit_solution(5027461933843266245)
XLA Ops:
  0.0 24.3 %all-to-all-start = ((f32[512,1,512]{2,1,0:T(1,128)}), f32[512,1,512]{2,1,0:T(1,128)S(1)}, u32[]{:S(2)}, u32[]{:S(2)}) async-start(f32[512,1,512]{2,1,0:T(1,128)} %bitcast.90), calls=%async_computation | async-start | bytes 2097152 | tf_op jit(solution)/shard_map/all_to_all | solution.py:51
  24.4 9.6 %fusion.31 = (f32[512,512]{1,0:T(8,128)}, f32[512,512]{1,0:T(8,128)}, f32[512,512]{1,0:T(8,128)S(1)}, f32[512,512]{1,0:T(8,128)S(1)}) fusion(s32[512]{0:T(512)S(1)} %get-tuple-element.49, s32[512]{0:T(512)S(1)} %get-tuple-element.48), kind=kLoop, calls=%fused_computation.51 | loop fusion | flops 8126464 | bytes 4198400 | tf_op jit(solution)/shard_map/sin | solution.py:24
  34.0 0.2 pad_maximum_fusion
  34.2 48.8 %all-to-all-done = f32[512,1,512]{2,1,0:T(1,128)S(1)} async-done(((f32[512,1,512]{2,1,0:T(1,128)}), f32[512,1,512]{2,1,0:T(1,128)S(1)}, u32[]{:S(2)}, u32[]{:S(2)}) %all-to-all-start) | async-done | bytes 1048608 | tf_op jit(solution)/shard_map/all_to_all | solution.py:51
  82.9 0.1 copy.32
  83.0 1.9 fusion.89
  84.9 0.0 copy-start.1
  84.9 0.0 copy-start.2
  84.9 0.4 fusion.88
  85.3 0.8 copy-done.1
  86.1 0.3 copy-done.2
  86.4 7.7 %multiply_add_fusion = f32[512,2,512]{2,1,0:T(2,128)} fusion(pred[2]{0:T(512)(128)(4,1)S(1)} %iota_compare_fusion, f32[512,512]{1,0:T(8,128)S(1)} %copy-done.1, f32[512,512]{1,0:T(8,128)S(1)} %get-tuple-element.36, f32[512,512]{1,0:T(8,128)S(1)} %copy-done.2, f32[512,512]{1,0:T(8,128)S(1)} %get-tuple-element.37, f32[512,512]{1,0:T(8,128)S(1)} %get-tuple-element.35), kind=kLoop, calls=%fused_computation.12 | loop fusion | flops 2621440 | bytes 7340034 | tf_op jit(solution)/shard_map/add | solution.py:68
  94.1 8.6 %all-to-all-start.1 = ((f32[512,2,512]{2,1,0:T(2,128)}), f32[512,2,512]{2,1,0:T(2,128)S(1)}, u32[]{:S(2)}, u32[]{:S(2)}) async-start(f32[512,2,512]{2,1,0:T(2,128)} %multiply_add_fusion), calls=%async_computation.1 | async-start | bytes 4194304 | tf_op jit(solution)/shard_map/all_to_all | solution.py:70
  102.7 0.1 fusion.70
  102.8 0.1 fusion.67
  102.9 0.1 fusion.68
  103.0 0.3 fusion.56
  103.3 0.1 fusion.62
  103.4 0.8 fusion.60
  104.2 0.6 pad_maximum_fusion.3
  104.8 0.3 fusion.48
  105.2 5.3 %fusion.29 = (f32[32,8192]{1,0:T(8,128)S(1)}, f32[32,8192]{1,0:T(8,128)}) fusion(), kind=kLoop, calls=%fused_computation.49 | loop fusion | flops 3670016 | bytes 2097152 | tf_op jit(solution)/shard_map/sin | solution.py:24
  110.5 93.3 %all-to-all-done.1 = f32[512,2,512]{2,1,0:T(2,128)S(1)} async-done(((f32[512,2,512]{2,1,0:T(2,128)}), f32[512,2,512]{2,1,0:T(2,128)S(1)}, u32[]{:S(2)}, u32[]{:S(2)}) %all-to-all-start.1) | async-done | bytes 2097184 | tf_op jit(solution)/shard_map/all_to_all | solution.py:70
  203.8 3.0 %fusion.9 = f32[2,32,16,512]{3,1,2,0:T(8,128)S(1)} fusion(f32[32,16,2,512]{3,2,1,0:T(2,128)S(1)} %bitcast.82, f32[2,2,32,32]{2,3,1,0:T(8,128)} %pad_maximum_fusion.3), kind=kOutput, calls=%fused_computation.16 | convolution fusion | flops 201326592 | bytes 4210688 | tf_op jit(solution)/shard_map/pqlm,lhqt->pmht/dot_general | solution.py:85
  206.8 0.3 fusion.87
  207.1 0.0 copy-start
  207.1 0.1 copy.19
  207.2 0.1 copy.20
  207.3 1.0 copy-done
  208.3 0.3 add_bitcast_fusion
  208.6 0.2 copy.21
  208.8 0.2 copy.22
  209.0 0.0 copy-start.3
  209.0 0.0 copy-start.4
  209.0 1.0 fusion.13
  210.1 0.0 copy-done.3
  210.1 0.0 copy-done.4
  210.1 0.4 multiply_add_fusion.1
  210.5 1.0 fusion.12
  211.5 1.5 copy.11
  (7 shorter events, 0.1 us)
Async XLA Ops:
  0.0 82.9 %all-to-all-start = ((f32[512,1,512]{2,1,0:T(1,128)}), f32[512,1,512]{2,1,0:T(1,128)S(1)}, u32[]{:S(2)}, u32[]{:S(2)}) async-start(f32[512,1,512]{2,1,0:T(1,128)} %bitcast.90), calls=%async_computation | async-start | bytes 2097152 | tf_op jit(solution)/shard_map/all_to_all | solution.py:51
  84.9 1.2 copy-start.1
  84.9 1.5 copy-start.2
  94.1 109.7 %all-to-all-start.1 = ((f32[512,2,512]{2,1,0:T(2,128)}), f32[512,2,512]{2,1,0:T(2,128)S(1)}, u32[]{:S(2)}, u32[]{:S(2)}) async-start(f32[512,2,512]{2,1,0:T(2,128)} %multiply_add_fusion), calls=%async_computation.1 | async-start | bytes 4194304 | tf_op jit(solution)/shard_map/all_to_all | solution.py:70
  207.1 1.2 copy-start
  209.0 1.1 copy-start.3
  209.0 1.1 copy-start.4

commit v12 on v10

--- a/solution.py
+++ b/solution.py
@@ -85,7 +85,11 @@
     values = jnp.stack(turn(values, *twiddle_b)).reshape(2, local_b, size_c, size_d)
     values = jnp.einsum("pqck,qmcd->pmkd", table_c, values, precision=PRECISE)
     values = jnp.stack(turn(values, twiddle_c[0][None], twiddle_c[1][None]))
-    values = jnp.einsum("pqdk,qmcd->pmck", table_d, values, precision=PRECISE)
+    parts = [
+        jnp.einsum("qdk,qmcd->mck", table_d[p], values, precision=PRECISE)[None] for p in range(2)
+    ]
+    first = lax.broadcasted_iota(jnp.int32, (2, local_b, size_c, size_d), 0) == 0
+    values = with_layout_constraint(jnp.where(first, *parts), Layout((0, 1, 2, 3)))
     return values.reshape(2, 1, 1, local_b, size_c, size_d)
 
 

time: 207 us -> 208 us (level)
  transfers between devices with their start and end apart: 2 -> 2, of which waited for: 2 -> 2; matrix products, arithmetic and copies ran while one was open for 9% -> 8% of each run, Pallas kernels for 0% -> 0%
where the time goes in v12:
time: 208 us
  waiting for transfers between devices  142 us (68%)
  starting transfers between devices  32.9 us (16%)
  other arithmetic  22.6 us (11%)
  matrix products  7.91 us (4%)
    all_to_all x1, waiting for transfers between devices, shards(): lax.all_to_all(section, DEVICES, split_axis=0, concat_axis=0, tiled=True)  93.3 us
    all_to_all x1, waiting for transfers between devices, shards(): lax.all_to_all(record.reshape(groups, columns), DEVICES, split_axis=0, co...  48.8 us
    all_to_all x1, starting transfers between devices, shards(): lax.all_to_all(record.reshape(groups, columns), DEVICES, split_axis=0, co...  24.3 us
    sin x6, other arithmetic, unit_turn(): return (jnp.cos(angles), jnp.sin(angles))  16.2 us
    all_to_all x1, starting transfers between devices, shards(): lax.all_to_all(section, DEVICES, split_axis=0, concat_axis=0, tiled=True)  8.56 us
  transfers between devices with their start and end apart: 2, of which 2 were waited for; matrix products, arithmetic and copies ran while one was open for 8% of the time, Pallas kernels for 0%

profile of v12, /device:TPU:1, one launch (start us, length us, event | category | flops | bytes accessed | tf_op | source)
XLA Modules:
  0.0 207.6 jit_solution(11020793313222760411)
XLA Ops:
  0.0 24.3 %all-to-all-start = ((f32[512,1,512]{2,1,0:T(1,128)}), f32[512,1,512]{2,1,0:T(1,128)S(1)}, u32[]{:S(2)}, u32[]{:S(2)}) async-start(f32[512,1,512]{2,1,0:T(1,128)} %bitcast.91), calls=%async_computation | async-start | bytes 2097152 | tf_op jit(solution)/shard_map/all_to_all | solution.py:51
  24.4 9.6 %fusion.31 = (f32[512,512]{1,0:T(8,128)}, f32[512,512]{1,0:T(8,128)}, f32[512,512]{1,0:T(8,128)S(1)}, f32[512,512]{1,0:T(8,128)S(1)}) fusion(s32[512]{0:T(512)S(1)} %get-tuple-element.48, s32[512]{0:T(512)S(1)} %get-tuple-element.47), kind=kLoop, calls=%fused_computation.54 | loop fusion | flops 8126464 | bytes 4198400 | tf_op jit(solution)/shard_map/sin | solution.py:24
  34.0 0.2 pad_maximum_fusion
  34.2 48.8 %all-to-all-done = f32[512,1,512]{2,1,0:T(1,128)S(1)} async-done(((f32[512,1,512]{2,1,0:T(1,128)}), f32[512,1,512]{2,1,0:T(1,128)S(1)}, u32[]{:S(2)}, u32[]{:S(2)}) %all-to-all-start) | async-done | bytes 1048608 | tf_op jit(solution)/shard_map/all_to_all | solution.py:51
  82.9 0.1 copy.32
  83.0 0.0 copy-start
  83.0 0.0 copy-start.1
  83.0 1.9 fusion.92
  84.9 0.0 copy-done
  84.9 0.0 copy-done.1
  84.9 0.5 multiply_add_fusion.1
  85.4 2.2 %broadcast_select_fusion = f32[512,2,512]{2,1,0:T(2,128)} fusion(pred[2]{0:T(512)(128)(4,1)S(1)} %iota_compare_fusion, f32[512,512]{1,0:T(8,128)S(1)} %get-tuple-element.32, f32[512,512]{1,0:T(8,128)S(1)} %get-tuple-element.31), kind=kLoop, calls=%fused_computation.10 | loop fusion | flops 524288 | bytes 4194306 | tf_op jit(solution)/shard_map/jit(_where)/select_n | solution.py:67
  87.6 8.6 %all-to-all-start.1 = ((f32[512,2,512]{2,1,0:T(2,128)}), f32[512,2,512]{2,1,0:T(2,128)S(1)}, u32[]{:S(2)}, u32[]{:S(2)}) async-start(f32[512,2,512]{2,1,0:T(2,128)} %broadcast_select_fusion), calls=%async_computation.1 | async-start | bytes 4194304 | tf_op jit(solution)/shard_map/all_to_all | solution.py:68
  96.2 0.1 fusion.73
  96.3 0.1 fusion.70
  96.4 0.1 fusion.71
  96.5 0.3 fusion.59
  96.8 0.1 fusion.65
  96.9 0.8 fusion.63
  97.7 0.6 pad_maximum_fusion.10
  98.3 0.3 fusion.51
  98.7 5.3 %fusion.29 = (f32[32,8192]{1,0:T(8,128)S(1)}, f32[32,8192]{1,0:T(8,128)}) fusion(), kind=kLoop, calls=%fused_computation.52 | loop fusion | flops 3670016 | bytes 2097152 | tf_op jit(solution)/shard_map/sin | solution.py:24
  104.0 93.3 %all-to-all-done.1 = f32[512,2,512]{2,1,0:T(2,128)S(1)} async-done(((f32[512,2,512]{2,1,0:T(2,128)}), f32[512,2,512]{2,1,0:T(2,128)S(1)}, u32[]{:S(2)}, u32[]{:S(2)}) %all-to-all-start.1) | async-done | bytes 2097184 | tf_op jit(solution)/shard_map/all_to_all | solution.py:68
  197.3 3.0 %fusion.8 = f32[2,32,16,512]{3,1,2,0:T(8,128)S(1)} fusion(f32[32,16,2,512]{3,2,1,0:T(2,128)S(1)} %bitcast.83, f32[2,2,32,32]{2,3,1,0:T(8,128)} %pad_maximum_fusion.10), kind=kOutput, calls=%fused_computation.16 | convolution fusion | flops 201326592 | bytes 4210688 | tf_op jit(solution)/shard_map/pqlm,lhqt->pmht/dot_general | solution.py:83
  200.3 0.3 fusion.91
  200.6 0.0 copy-start.2
  200.6 0.1 copy.19
  200.7 0.1 copy.20
  200.8 1.0 copy-done.2
  201.8 0.3 add_bitcast_fusion
  202.1 0.2 copy.21
  202.3 0.2 copy.22
  202.5 0.0 copy-start.3
  202.5 0.0 copy-start.4
  202.5 1.0 fusion.11
  203.6 0.0 copy-done.3
  203.6 0.0 copy-done.4
  203.6 0.4 multiply_add_fusion
  204.0 1.0 fusion.12
  205.0 1.0 fusion.13
  206.0 1.6 select_bitcast_fusion
  (7 shorter events, 0.1 us)
Async XLA Ops:
  0.0 82.9 %all-to-all-start = ((f32[512,1,512]{2,1,0:T(1,128)}), f32[512,1,512]{2,1,0:T(1,128)S(1)}, u32[]{:S(2)}, u32[]{:S(2)}) async-start(f32[512,1,512]{2,1,0:T(1,128)} %bitcast.91), calls=%async_computation | async-start | bytes 2097152 | tf_op jit(solution)/shard_map/all_to_all | solution.py:51
  83.0 1.9 copy-start
  83.0 1.9 copy-start.1
  87.6 109.7 %all-to-all-start.1 = ((f32[512,2,512]{2,1,0:T(2,128)}), f32[512,2,512]{2,1,0:T(2,128)S(1)}, u32[]{:S(2)}, u32[]{:S(2)}) async-start(f32[512,2,512]{2,1,0:T(2,128)} %broadcast_select_fusion), calls=%async_computation.1 | async-start | bytes 4194304 | tf_op jit(solution)/shard_map/all_to_all | solution.py:68
  200.6 1.2 copy-start.2
  202.5 1.1 copy-start.3
  202.5 1.1 copy-start.4

commit v13 on v10

--- a/solution.py
+++ b/solution.py
@@ -69,20 +69,23 @@
 
     index_b = jnp.arange(local_b, dtype=jnp.int32)
     table_b = block_table(index_b, index_b, local_b, 1.0)
-    inner = jnp.arange(size_c * size_d, dtype=jnp.int32)
-    twiddle_b = unit_turn(index_b[:, None] * inner[None, :] % column_count, column_count)
     index_c = jnp.arange(size_c, dtype=jnp.int32)
+    index_d = jnp.arange(size_d, dtype=jnp.int32)
+    coarse = unit_turn(index_b[:, None] * (index_c * size_d)[None, :] % column_count, column_count)
+    fine = unit_turn(index_b[:, None] * index_d[None, :] % column_count, column_count)
     table_c = block_table(index_c, index_c, size_c, 1.0)
-    index_d = jnp.arange(size_d, dtype=jnp.int32)
     twiddle_c = unit_turn(index_c[:, None] * index_d[None, :] % (size_c * size_d), size_c * size_d)
     table_d = block_table(index_d, index_d, size_d, 1.0)
-    owned, table_b, twiddle_b, table_c, twiddle_c, table_d = lax.optimization_barrier(
-        (owned, table_b, twiddle_b, table_c, twiddle_c, table_d)
+    owned, table_b, coarse, fine, table_c, twiddle_c, table_d = lax.optimization_barrier(
+        (owned, table_b, coarse, fine, table_c, twiddle_c, table_d)
     )
     values = owned.reshape(local_b, groups // local_b, 2, columns)
     values = jnp.einsum("pqlm,lhqt->pmht", table_b, values, precision=PRECISE)
-    values = values.reshape(2, local_b, size_c * size_d)
-    values = jnp.stack(turn(values, *twiddle_b)).reshape(2, local_b, size_c, size_d)
+    values = values.reshape(2, local_b, size_c, size_d)
+    cos_c, sin_c = coarse[0][:, :, None], coarse[1][:, :, None]
+    cos_d, sin_d = fine[0][:, None, :], fine[1][:, None, :]
+    twiddle_b = (cos_c * cos_d - sin_c * sin_d, sin_c * cos_d + cos_c * sin_d)
+    values = jnp.stack(turn(values, *twiddle_b))
     values = jnp.einsum("pqck,qmcd->pmkd", table_c, values, precision=PRECISE)
     values = jnp.stack(turn(values, twiddle_c[0][None], twiddle_c[1][None]))
     values = jnp.einsum("pqdk,qmcd->pmck", table_d, values, precision=PRECISE)

time: 207 us -> 207 us (level)
  waiting for transfers between devices: 142 us -> 147 us
  other arithmetic: 21 us -> 17.6 us
    all_to_all x1, waiting for transfers between devices: 93.3 us -> 97.8 us  [shards(): lax.all_to_all(section, DEVICES, split_axis=0, concat_axis=0, tiled=True)]
    sin x6 -> x7, other arithmetic: 16.2 us -> 12.3 us  [unit_turn(): return (jnp.cos(angles), jnp.sin(angles))]
  transfers between devices with their start and end apart: 2 -> 2, of which waited for: 2 -> 2; matrix products, arithmetic and copies ran while one was open for 9% -> 6% of each run, Pallas kernels for 0% -> 0%
where the time goes in v13:
time: 207 us
  waiting for transfers between devices  147 us (71%)
  starting transfers between devices  32.9 us (16%)
  other arithmetic  17.6 us (9%)
  matrix products  6.07 us (3%)
  local copies, waits for them, and re-layouts  3.15 us (2%)
    all_to_all x1, waiting for transfers between devices, shards(): lax.all_to_all(section, DEVICES, split_axis=0, concat_axis=0, tiled=True)  97.8 us
    all_to_all x1, waiting for transfers between devices, shards(): lax.all_to_all(record.reshape(groups, columns), DEVICES, split_axis=0, co...  48.8 us
    all_to_all x1, starting transfers between devices, shards(): lax.all_to_all(record.reshape(groups, columns), DEVICES, split_axis=0, co...  24.3 us
    sin x7, other arithmetic, unit_turn(): return (jnp.cos(angles), jnp.sin(angles))  12.3 us
    all_to_all x1, starting transfers between devices, shards(): lax.all_to_all(section, DEVICES, split_axis=0, concat_axis=0, tiled=True)  8.56 us
  transfers between devices with their start and end apart: 2, of which 2 were waited for; matrix products, arithmetic and copies ran while one was open for 6% of the time, Pallas kernels for 0%

profile of v13, /device:TPU:1, one launch (start us, length us, event | category | flops | bytes accessed | tf_op | source)
XLA Modules:
  0.0 206.6 jit_solution(6294151943223041812)
XLA Ops:
  0.0 24.3 %all-to-all-start = ((f32[512,1,512]{2,1,0:T(1,128)}), f32[512,1,512]{2,1,0:T(1,128)S(1)}, u32[]{:S(2)}, u32[]{:S(2)}) async-start(f32[512,1,512]{2,1,0:T(1,128)} %bitcast.86), calls=%async_computation | async-start | bytes 2097152 | tf_op jit(solution)/shard_map/all_to_all | solution.py:51
  24.4 9.6 %fusion.25 = (f32[512,512]{1,0:T(8,128)}, f32[512,512]{1,0:T(8,128)}, f32[512,512]{1,0:T(8,128)S(1)}, f32[512,512]{1,0:T(8,128)S(1)}) fusion(s32[512]{0:T(512)S(1)} %get-tuple-element.54, s32[512]{0:T(512)S(1)} %get-tuple-element.53), kind=kLoop, calls=%fused_computation.48 | loop fusion | flops 8126464 | bytes 4198400 | tf_op jit(solution)/shard_map/sin | solution.py:24
  34.0 0.2 pad_maximum_fusion
  34.2 48.8 %all-to-all-done = f32[512,1,512]{2,1,0:T(1,128)S(1)} async-done(((f32[512,1,512]{2,1,0:T(1,128)}), f32[512,1,512]{2,1,0:T(1,128)S(1)}, u32[]{:S(2)}, u32[]{:S(2)}) %all-to-all-start) | async-done | bytes 1048608 | tf_op jit(solution)/shard_map/all_to_all | solution.py:51
  82.9 0.1 copy.34
  83.0 0.0 copy-start
  83.0 0.0 copy-start.1
  83.0 1.9 fusion.98
  84.9 0.0 copy-done
  84.9 0.0 copy-done.1
  84.9 0.5 multiply_add_fusion.2
  85.4 2.2 %broadcast_select_fusion = f32[512,2,512]{2,1,0:T(2,128)} fusion(pred[2]{0:T(512)(128)(4,1)S(1)} %iota_compare_fusion, f32[512,512]{1,0:T(8,128)S(1)} %get-tuple-element.34, f32[512,512]{1,0:T(8,128)S(1)} %get-tuple-element.33), kind=kLoop, calls=%fused_computation.12 | loop fusion | flops 524288 | bytes 4194306 | tf_op jit(solution)/shard_map/jit(_where)/select_n | solution.py:67
  87.6 8.6 %all-to-all-start.1 = ((f32[512,2,512]{2,1,0:T(2,128)}), f32[512,2,512]{2,1,0:T(2,128)S(1)}, u32[]{:S(2)}, u32[]{:S(2)}) async-start(f32[512,2,512]{2,1,0:T(2,128)} %broadcast_select_fusion), calls=%async_computation.1 | async-start | bytes 4194304 | tf_op jit(solution)/shard_map/all_to_all | solution.py:68
  96.2 0.1 fusion.80
  96.3 0.1 fusion.73
  96.4 0.1 fusion.78
  96.5 0.7 fusion.74
  97.2 0.3 fusion.50
  97.5 0.1 fusion.62
  97.6 0.8 fusion.60
  98.4 0.3 fusion.42
  98.8 0.7 fusion.76
  99.5 97.8 %all-to-all-done.1 = f32[512,2,512]{2,1,0:T(2,128)S(1)} async-done(((f32[512,2,512]{2,1,0:T(2,128)}), f32[512,2,512]{2,1,0:T(2,128)S(1)}, u32[]{:S(2)}, u32[]{:S(2)}) %all-to-all-start.1) | async-done | bytes 2097184 | tf_op jit(solution)/shard_map/all_to_all | solution.py:68
  197.3 2.2 %fusion.9 = f32[2,32,16,512]{3,1,2,0:T(8,128)S(1)} fusion(f32[32,16,2,512]{3,2,1,0:T(2,128)S(1)} %bitcast.84, f32[2,2,32,32]{2,3,1,0:T(8,128)S(1)} %pad_maximum_fusion.3), kind=kOutput, calls=%fused_computation.16 | convolution fusion | flops 201326592 | bytes 4210688 | tf_op jit(solution)/shard_map/pqlm,lhqt->pmht/dot_general | solution.py:83
  199.5 0.2 fusion.97
  199.7 0.6 copy.13
  200.3 0.1 squeeze.4
  200.4 0.6 copy.15
  201.0 0.1 squeeze.5
  201.1 1.5 fusion.20
  202.6 0.0 copy-start.2
  202.6 0.0 copy-start.3
  202.6 1.0 fusion.13
  203.7 0.0 copy-done.2
  203.7 0.0 copy-done.3
  203.7 0.4 multiply_add_fusion
  204.1 1.0 fusion.12
  205.1 1.5 copy.19
  (9 shorter events, 0.1 us)
Async XLA Ops:
  0.0 82.9 %all-to-all-start = ((f32[512,1,512]{2,1,0:T(1,128)}), f32[512,1,512]{2,1,0:T(1,128)S(1)}, u32[]{:S(2)}, u32[]{:S(2)}) async-start(f32[512,1,512]{2,1,0:T(1,128)} %bitcast.86), calls=%async_computation | async-start | bytes 2097152 | tf_op jit(solution)/shard_map/all_to_all | solution.py:51
  83.0 1.9 copy-start
  83.0 1.9 copy-start.1
  87.6 109.7 %all-to-all-start.1 = ((f32[512,2,512]{2,1,0:T(2,128)}), f32[512,2,512]{2,1,0:T(2,128)S(1)}, u32[]{:S(2)}, u32[]{:S(2)}) async-start(f32[512,2,512]{2,1,0:T(2,128)} %broadcast_select_fusion), calls=%async_computation.1 | async-start | bytes 4194304 | tf_op jit(solution)/shard_map/all_to_all | solution.py:68
  202.6 1.1 copy-start.2
  202.6 1.1 copy-start.3

commit v14 on v10

--- a/solution.py
+++ b/solution.py
@@ -85,7 +85,7 @@
     values = jnp.stack(turn(values, *twiddle_b)).reshape(2, local_b, size_c, size_d)
     values = jnp.einsum("pqck,qmcd->pmkd", table_c, values, precision=PRECISE)
     values = jnp.stack(turn(values, twiddle_c[0][None], twiddle_c[1][None]))
-    values = jnp.einsum("pqdk,qmcd->pmck", table_d, values, precision=PRECISE)
+    values = jnp.einsum("qmcd,pqdk->pmck", values, table_d, precision=PRECISE)
     return values.reshape(2, 1, 1, local_b, size_c, size_d)
 
 

time: 207 us -> 207 us (level)
  no operation moved by 1% of the time
where the time goes in v14:
time: 207 us; the launch traced here: 206 us
  waiting for transfers between devices  142 us (69%)
  starting transfers between devices  32.9 us (16%)
  other arithmetic  21 us (10%)
  matrix products  8.28 us (4%)
    all_to_all x1, waiting for transfers between devices, shards(): lax.all_to_all(section, DEVICES, split_axis=0, concat_axis=0, tiled=True)  93.3 us
    all_to_all x1, waiting for transfers between devices, shards(): lax.all_to_all(record.reshape(groups, columns), DEVICES, split_axis=0, co...  48.8 us
    all_to_all x1, starting transfers between devices, shards(): lax.all_to_all(record.reshape(groups, columns), DEVICES, split_axis=0, co...  24.3 us
    sin x6, other arithmetic, unit_turn(): return (jnp.cos(angles), jnp.sin(angles))  16.2 us
    all_to_all x1, starting transfers between devices, shards(): lax.all_to_all(section, DEVICES, split_axis=0, concat_axis=0, tiled=True)  8.56 us
  transfers between devices with their start and end apart: 2, of which 2 were waited for; matrix products, arithmetic and copies ran while one was open for 9% of the time, Pallas kernels for 0%

profile of v14, /device:TPU:1, one launch (start us, length us, event | category | flops | bytes accessed | tf_op | source)
XLA Modules:
  0.0 206.4 jit_solution(9494562246063230322)
XLA Ops:
  0.0 24.3 %all-to-all-start = ((f32[512,1,512]{2,1,0:T(1,128)}), f32[512,1,512]{2,1,0:T(1,128)S(1)}, u32[]{:S(2)}, u32[]{:S(2)}) async-start(f32[512,1,512]{2,1,0:T(1,128)} %bitcast.92), calls=%async_computation | async-start | bytes 2097152 | tf_op jit(solution)/shard_map/all_to_all | solution.py:51
  24.4 9.6 %fusion.31 = (f32[512,512]{1,0:T(8,128)}, f32[512,512]{1,0:T(8,128)}, f32[512,512]{1,0:T(8,128)S(1)}, f32[512,512]{1,0:T(8,128)S(1)}) fusion(s32[512]{0:T(512)S(1)} %get-tuple-element.48, s32[512]{0:T(512)S(1)} %get-tuple-element.47), kind=kLoop, calls=%fused_computation.53 | loop fusion | flops 8126464 | bytes 4198400 | tf_op jit(solution)/shard_map/sin | solution.py:24
  34.0 0.2 pad_maximum_fusion
  34.2 48.8 %all-to-all-done = f32[512,1,512]{2,1,0:T(1,128)S(1)} async-done(((f32[512,1,512]{2,1,0:T(1,128)}), f32[512,1,512]{2,1,0:T(1,128)S(1)}, u32[]{:S(2)}, u32[]{:S(2)}) %all-to-all-start) | async-done | bytes 1048608 | tf_op jit(solution)/shard_map/all_to_all | solution.py:51
  82.9 0.1 copy.32
  83.0 0.0 copy-start
  83.0 0.0 copy-start.1
  83.0 1.9 fusion.88
  84.9 0.0 copy-done
  84.9 0.0 copy-done.1
  84.9 0.5 multiply_add_fusion.1
  85.4 2.2 %broadcast_select_fusion = f32[512,2,512]{2,1,0:T(2,128)} fusion(pred[2]{0:T(512)(128)(4,1)S(1)} %iota_compare_fusion, f32[512,512]{1,0:T(8,128)S(1)} %get-tuple-element.32, f32[512,512]{1,0:T(8,128)S(1)} %get-tuple-element.31), kind=kLoop, calls=%fused_computation.12 | loop fusion | flops 524288 | bytes 4194306 | tf_op jit(solution)/shard_map/jit(_where)/select_n | solution.py:67
  87.6 8.6 %all-to-all-start.1 = ((f32[512,2,512]{2,1,0:T(2,128)}), f32[512,2,512]{2,1,0:T(2,128)S(1)}, u32[]{:S(2)}, u32[]{:S(2)}) async-start(f32[512,2,512]{2,1,0:T(2,128)} %broadcast_select_fusion), calls=%async_computation.1 | async-start | bytes 4194304 | tf_op jit(solution)/shard_map/all_to_all | solution.py:68
  96.2 0.1 fusion.70
  96.3 0.1 fusion.67
  96.4 0.1 fusion.68
  96.5 0.3 fusion.56
  96.8 0.1 fusion.62
  96.9 0.8 fusion.60
  97.7 0.6 pad_maximum_fusion.3
  98.3 0.3 fusion.48
  98.7 5.3 %fusion.29 = (f32[32,8192]{1,0:T(8,128)S(1)}, f32[32,8192]{1,0:T(8,128)}) fusion(), kind=kLoop, calls=%fused_computation.51 | loop fusion | flops 3670016 | bytes 2097152 | tf_op jit(solution)/shard_map/sin | solution.py:24
  104.0 93.3 %all-to-all-done.1 = f32[512,2,512]{2,1,0:T(2,128)S(1)} async-done(((f32[512,2,512]{2,1,0:T(2,128)}), f32[512,2,512]{2,1,0:T(2,128)S(1)}, u32[]{:S(2)}, u32[]{:S(2)}) %all-to-all-start.1) | async-done | bytes 2097184 | tf_op jit(solution)/shard_map/all_to_all | solution.py:68
  197.3 3.0 %fusion.9 = f32[2,32,16,512]{3,1,2,0:T(8,128)S(1)} fusion(f32[32,16,2,512]{3,2,1,0:T(2,128)S(1)} %bitcast.84, f32[2,2,32,32]{2,3,1,0:T(8,128)} %pad_maximum_fusion.3), kind=kOutput, calls=%fused_computation.16 | convolution fusion | flops 201326592 | bytes 4210688 | tf_op jit(solution)/shard_map/pqlm,lhqt->pmht/dot_general | solution.py:83
  200.3 0.3 fusion.87
  200.6 0.0 copy-start.2
  200.6 0.1 copy.19
  200.7 0.1 copy.20
  200.8 1.0 copy-done.2
  201.8 0.3 add_bitcast_fusion
  202.1 0.2 copy.21
  202.3 0.2 copy.22
  202.5 0.0 copy-start.3
  202.5 0.0 copy-start.4
  202.5 1.0 fusion.13
  203.6 0.0 copy-done.3
  203.6 0.0 copy-done.4
  203.6 0.4 multiply_add_fusion
  204.0 2.4 %fusion.12 = f32[2,1,1,32,64,128]{5,4,3,2,1,0:T(8,128)} fusion(f32[1,32,64,128]{3,2,0,1:T(8,128)S(1)} %get-tuple-element.34, f32[1,32,64,128]{3,2,0,1:T(8,128)S(1)} %get-tuple-element.33, f32[2,2,128,128]{3,2,1,0:T(8,128)S(1)} %pad_maximum_fusion.1), kind=kOutput, calls=%fused_computation.17 | convolution fusion | flops 805830656 | bytes 4456448 | tf_op jit(solution)/shard_map/qmcd,pqdk->pmck/dot_general | solution.py:88
  (7 shorter events, 0.1 us)
Async XLA Ops:
  0.0 82.9 %all-to-all-start = ((f32[512,1,512]{2,1,0:T(1,128)}), f32[512,1,512]{2,1,0:T(1,128)S(1)}, u32[]{:S(2)}, u32[]{:S(2)}) async-start(f32[512,1,512]{2,1,0:T(1,128)} %bitcast.92), calls=%async_computation | async-start | bytes 2097152 | tf_op jit(solution)/shard_map/all_to_all | solution.py:51
  83.0 1.9 copy-start
  83.0 1.9 copy-start.1
  87.6 109.7 %all-to-all-start.1 = ((f32[512,2,512]{2,1,0:T(2,128)}), f32[512,2,512]{2,1,0:T(2,128)S(1)}, u32[]{:S(2)}, u32[]{:S(2)}) async-start(f32[512,2,512]{2,1,0:T(2,128)} %broadcast_select_fusion), calls=%async_computation.1 | async-start | bytes 4194304 | tf_op jit(solution)/shard_map/all_to_all | solution.py:68
  200.6 1.2 copy-start.2
  202.5 1.1 copy-start.3
  202.5 1.1 copy-start.4

commit v15 on v14

--- a/solution.py
+++ b/solution.py
@@ -83,7 +83,7 @@
     values = jnp.einsum("pqlm,lhqt->pmht", table_b, values, precision=PRECISE)
     values = values.reshape(2, local_b, size_c * size_d)
     values = jnp.stack(turn(values, *twiddle_b)).reshape(2, local_b, size_c, size_d)
-    values = jnp.einsum("pqck,qmcd->pmkd", table_c, values, precision=PRECISE)
+    values = jnp.einsum("qmcd,pqck->pmkd", values, table_c, precision=PRECISE)
     values = jnp.stack(turn(values, twiddle_c[0][None], twiddle_c[1][None]))
     values = jnp.einsum("qmcd,pqdk->pmck", values, table_d, precision=PRECISE)
     return values.reshape(2, 1, 1, local_b, size_c, size_d)

time: 207 us -> 207 us (level)
  no operation moved by 1% of the time
where the time goes in v15:
time: 207 us; the launch traced here: 206 us
  waiting for transfers between devices  142 us (69%)
  starting transfers between devices  32.9 us (16%)
  other arithmetic  21 us (10%)
  matrix products  8.35 us (4%)
    all_to_all x1, waiting for transfers between devices, shards(): lax.all_to_all(section, DEVICES, split_axis=0, concat_axis=0, tiled=True)  93.3 us
    all_to_all x1, waiting for transfers between devices, shards(): lax.all_to_all(record.reshape(groups, columns), DEVICES, split_axis=0, co...  48.8 us
    all_to_all x1, starting transfers between devices, shards(): lax.all_to_all(record.reshape(groups, columns), DEVICES, split_axis=0, co...  24.3 us
    sin x6, other arithmetic, unit_turn(): return (jnp.cos(angles), jnp.sin(angles))  16.2 us
    all_to_all x1, starting transfers between devices, shards(): lax.all_to_all(section, DEVICES, split_axis=0, concat_axis=0, tiled=True)  8.56 us
  transfers between devices with their start and end apart: 2, of which 2 were waited for; matrix products, arithmetic and copies ran while one was open for 9% of the time, Pallas kernels for 0%

profile of v15, /device:TPU:1, one launch (start us, length us, event | category | flops | bytes accessed | tf_op | source)
XLA Modules:
  0.0 206.4 jit_solution(8502564926887496767)
XLA Ops:
  0.0 24.3 %all-to-all-start = ((f32[512,1,512]{2,1,0:T(1,128)}), f32[512,1,512]{2,1,0:T(1,128)S(1)}, u32[]{:S(2)}, u32[]{:S(2)}) async-start(f32[512,1,512]{2,1,0:T(1,128)} %bitcast.92), calls=%async_computation | async-start | bytes 2097152 | tf_op jit(solution)/shard_map/all_to_all | solution.py:51
  24.4 9.6 %fusion.33 = (f32[512,512]{1,0:T(8,128)}, f32[512,512]{1,0:T(8,128)}, f32[512,512]{1,0:T(8,128)S(1)}, f32[512,512]{1,0:T(8,128)S(1)}) fusion(s32[512]{0:T(512)S(1)} %get-tuple-element.48, s32[512]{0:T(512)S(1)} %get-tuple-element.47), kind=kLoop, calls=%fused_computation.53 | loop fusion | flops 8126464 | bytes 4198400 | tf_op jit(solution)/shard_map/sin | solution.py:24
  34.0 0.2 pad_maximum_fusion
  34.2 48.8 %all-to-all-done = f32[512,1,512]{2,1,0:T(1,128)S(1)} async-done(((f32[512,1,512]{2,1,0:T(1,128)}), f32[512,1,512]{2,1,0:T(1,128)S(1)}, u32[]{:S(2)}, u32[]{:S(2)}) %all-to-all-start) | async-done | bytes 1048608 | tf_op jit(solution)/shard_map/all_to_all | solution.py:51
  82.9 0.1 copy.41
  83.0 0.0 copy-start
  83.0 0.0 copy-start.1
  83.0 1.9 fusion.89
  84.9 0.0 copy-done
  84.9 0.0 copy-done.1
  84.9 0.5 multiply_add_fusion.1
  85.4 2.2 %broadcast_select_fusion = f32[512,2,512]{2,1,0:T(2,128)} fusion(pred[2]{0:T(512)(128)(4,1)S(1)} %iota_compare_fusion, f32[512,512]{1,0:T(8,128)S(1)} %get-tuple-element.32, f32[512,512]{1,0:T(8,128)S(1)} %get-tuple-element.31), kind=kLoop, calls=%fused_computation.12 | loop fusion | flops 524288 | bytes 4194306 | tf_op jit(solution)/shard_map/jit(_where)/select_n | solution.py:67
  87.6 8.6 %all-to-all-start.1 = ((f32[512,2,512]{2,1,0:T(2,128)}), f32[512,2,512]{2,1,0:T(2,128)S(1)}, u32[]{:S(2)}, u32[]{:S(2)}) async-start(f32[512,2,512]{2,1,0:T(2,128)} %broadcast_select_fusion), calls=%async_computation.1 | async-start | bytes 4194304 | tf_op jit(solution)/shard_map/all_to_all | solution.py:68
  96.2 0.1 fusion.72
  96.3 0.1 fusion.69
  96.4 0.1 fusion.70
  96.5 0.3 fusion.58
  96.8 0.1 fusion.64
  96.9 0.8 fusion.62
  97.7 0.6 pad_maximum_fusion.4
  98.3 0.3 fusion.50
  98.7 5.3 %fusion.31 = (f32[32,8192]{1,0:T(8,128)S(1)}, f32[32,8192]{1,0:T(8,128)}) fusion(), kind=kLoop, calls=%fused_computation.51 | loop fusion | flops 3670016 | bytes 2097152 | tf_op jit(solution)/shard_map/sin | solution.py:24
  104.0 93.3 %all-to-all-done.1 = f32[512,2,512]{2,1,0:T(2,128)S(1)} async-done(((f32[512,2,512]{2,1,0:T(2,128)}), f32[512,2,512]{2,1,0:T(2,128)S(1)}, u32[]{:S(2)}, u32[]{:S(2)}) %all-to-all-start.1) | async-done | bytes 2097184 | tf_op jit(solution)/shard_map/all_to_all | solution.py:68
  197.3 3.0 %fusion.9 = f32[2,32,16,512]{3,1,2,0:T(8,128)S(1)} fusion(f32[32,16,2,512]{3,2,1,0:T(2,128)S(1)} %bitcast.84, f32[2,2,32,32]{2,3,1,0:T(8,128)} %pad_maximum_fusion.4), kind=kOutput, calls=%fused_computation.16 | convolution fusion | flops 201326592 | bytes 4210688 | tf_op jit(solution)/shard_map/pqlm,lhqt->pmht/dot_general | solution.py:83
  200.3 0.3 fusion.88
  200.6 0.0 copy-start.2
  200.6 0.1 copy.22
  200.7 0.1 copy.23
  200.8 1.0 copy-done.2
  201.8 0.3 add_bitcast_fusion
  202.1 0.2 copy.24
  202.3 0.2 copy.25
  202.5 0.0 copy-start.3
  202.5 0.0 copy-start.4
  202.5 1.1 fusion.12
  203.6 0.0 copy-done.3
  203.6 0.0 copy-done.4
  203.6 0.4 multiply_add_fusion
  204.1 2.4 %fusion.13 = f32[2,1,1,32,64,128]{5,4,3,2,1,0:T(8,128)} fusion(f32[2,2,128,128]{3,2,1,0:T(8,128)S(1)} %pad_maximum_fusion.2, f32[1,32,64,128]{3,2,1,0:T(8,128)S(1)} %get-tuple-element.34, f32[1,32,64,128]{3,2,1,0:T(8,128)S(1)} %get-tuple-element.33), kind=kOutput, calls=%fused_computation.18 | convolution fusion | flops 805830656 | bytes 4456448 | tf_op jit(solution)/shard_map/qmcd,pqdk->pmck/dot_general | solution.py:88
  (7 shorter events, 0.1 us)
Async XLA Ops:
  0.0 82.9 %all-to-all-start = ((f32[512,1,512]{2,1,0:T(1,128)}), f32[512,1,512]{2,1,0:T(1,128)S(1)}, u32[]{:S(2)}, u32[]{:S(2)}) async-start(f32[512,1,512]{2,1,0:T(1,128)} %bitcast.92), calls=%async_computation | async-start | bytes 2097152 | tf_op jit(solution)/shard_map/all_to_all | solution.py:51
  83.0 1.9 copy-start
  83.0 1.9 copy-start.1
  87.6 109.7 %all-to-all-start.1 = ((f32[512,2,512]{2,1,0:T(2,128)}), f32[512,2,512]{2,1,0:T(2,128)S(1)}, u32[]{:S(2)}, u32[]{:S(2)}) async-start(f32[512,2,512]{2,1,0:T(2,128)} %broadcast_select_fusion), calls=%async_computation.1 | async-start | bytes 4194304 | tf_op jit(solution)/shard_map/all_to_all | solution.py:68
  200.6 1.2 copy-start.2
  202.5 1.1 copy-start.3
  202.5 1.1 copy-start.4
